TPU v7x, 256 devices: a whole 4x4x8 slice. The times are simulated.
256 devices in a mesh: seq: 64 (over y, z, core), pb: 4 (over x).
Axes of the slice: x: 4, y: 4, z: 8, core: 2. Of those that a mesh axis runs over, the one named last changes fastest.
Arguments:
- tokens: bfloat16 [16384, 2048], P('seq'), may hold values from -0.119628906 to 0.119628906
- w_query: bfloat16 [2048, 2048], P(None, 'pb')
- w_key: bfloat16 [2048, 2048], P(None, 'pb')
- w_value: bfloat16 [2048, 2048], P(None, 'pb'), may hold values from -0.125 to 0.125
- w_out: bfloat16 [2048, 2048], P('pb'), may hold values from -0.125 to 0.125
- gain_attn: float32 [2048], replicated, may hold values from 0.1 to 1.9
- gain_embed: float32 [2048], replicated, may hold values from 0.1 to 1.9
- queries: bfloat16 [256, 32, 2048], P(('seq', 'pb')), may hold values from -0.125 to 0.125
- query_lengths: int32 [256], P(('seq', 'pb')), may hold values from 8 to 32
- group_lengths: int32 [128], replicated, may hold values from 1 to 1024, 16384 in all
- teacher: float32 [256, 128], P(('seq', 'pb')), may hold values from -12 to 12
Outputs:
- embedded: bfloat16 [16384, 2048], P('seq')
- scores: float32 [256, 128], P(('seq', 'pb'))
- score_gradient: float32 [256, 128], P(('seq', 'pb'))
- distill_loss: float32 [], replicated
Inputs may be any that keep to these rules, and one draw needn't show every extreme that they name: `group_lengths`: the groups cover the document in order: the lengths sum to 16384.
All inputs are finite; a program needn't handle non-finite values.
Results may differ from a plain program's by a relative error of at most 0.013.
Values may be sent and summed in bfloat16 or wider, within the bound.
No kernel may reach another device: no remote copies, remote signals or barrier semaphores. Data moves between devices by JAX's collectives and lax.ppermute only.
A program may use at most 128 MiB of HBM per device.

v0:
```python
import jax
import jax.numpy as jnp
from jax import lax
from jax.sharding import PartitionSpec as P

HD = 128
WIN = 2048
LQ = 32


EPSILON = 1e-06
SOFTMAX_TEMP = 0.1


def shifted_2(x, axis, by):
    count = lax.axis_size(axis)
    pairs = [(i, i + by) for i in range(count) if 0 <= i + by < count]
    return lax.ppermute(x, axis, pairs)


def rms_scale(values, gain):
    mean_sq = jnp.mean(values * values, axis=-1, keepdims=True)
    return values * lax.rsqrt(mean_sq + EPSILON) * gain


def segmented_max(values, group_id):
    span_len = values.shape[-1]
    stride = 1
    while stride < span_len:
        filler = jnp.full(values.shape[:-1] + (stride,), -jnp.inf, values.dtype)
        shifted = jnp.concatenate([filler, values[..., :-stride]], axis=-1)
        prior_id = jnp.concatenate([jnp.full((stride,), -1, jnp.int32), group_id[:-stride]])
        values = jnp.where((prior_id == group_id)[None, :], jnp.maximum(values, shifted), values)
        stride = stride * 2
    return values


def per_device(
    tokens,
    w_query,
    w_key,
    w_value,
    w_out,
    gain_attn,
    gain_embed,
    queries,
    query_lengths,
    group_lengths,
    teacher,
):
    shard_rows = tokens.shape[0]
    seq_count = lax.axis_size("seq")
    seq_place = lax.axis_index("seq")
    head_width = w_query.shape[1]
    heads_here = head_width // HD
    half_win = WIN // 2
    reach_count = half_win // shard_rows
    my_start = seq_place * shard_rows
    total_tokens = shard_rows * seq_count
    residual = tokens.astype(jnp.float32)
    normed = rms_scale(residual, gain_attn).astype(jnp.bfloat16)
    q_local = jnp.dot(normed, w_query, preferred_element_type=jnp.float32).astype(jnp.bfloat16)
    k_local = jnp.dot(normed, w_key, preferred_element_type=jnp.float32).astype(jnp.bfloat16)
    v_local = jnp.dot(normed, w_value, preferred_element_type=jnp.float32).astype(jnp.bfloat16)
    key_value = jnp.stack([k_local, v_local])
    earlier = [shifted_2(key_value, "seq", distance) for distance in range(reach_count, 0, -1)]
    later = [shifted_2(key_value, "seq", -distance) for distance in range(1, reach_count + 1)]
    window = jnp.concatenate(earlier + [key_value] + later, axis=1)
    span_rows = window.shape[1]
    q_pos = my_start + jnp.arange(shard_rows, dtype=jnp.int32)
    k_pos = my_start - reach_count * shard_rows + jnp.arange(span_rows, dtype=jnp.int32)
    in_window = (
        (jnp.abs(q_pos[:, None] - k_pos[None, :]) <= half_win)
        & (k_pos >= 0)[None, :]
        & (k_pos < total_tokens)[None, :]
    )
    q_heads = q_local.reshape(shard_rows, heads_here, HD)
    k_heads = window[0].reshape(span_rows, heads_here, HD)
    v_heads = window[1].reshape(span_rows, heads_here, HD)
    logits = jnp.einsum(
        "qhd,khd->hqk", q_heads, k_heads, preferred_element_type=jnp.float32
    ) * HD ** (-0.5)
    logits = jnp.where(in_window[None], logits, -jnp.inf)
    row_max = jnp.max(logits, axis=-1, keepdims=True)
    exp_terms = jnp.exp(logits - row_max)
    weights = (exp_terms / jnp.sum(exp_terms, axis=-1, keepdims=True)).astype(jnp.bfloat16)
    mixed = jnp.einsum("hqk,khd->qhd", weights, v_heads, preferred_element_type=jnp.float32)
    mixed = mixed.reshape(shard_rows, head_width).astype(jnp.bfloat16)
    partial_value = jnp.dot(mixed, w_out, preferred_element_type=jnp.float32)
    attn_sum = lax.psum(partial_value, "pb")
    embedded = rms_scale(residual + attn_sum, gain_embed).astype(jnp.bfloat16)
    group_end = jnp.cumsum(group_lengths)
    group_start = group_end - group_lengths
    group_id = jnp.sum((group_end[None, :] <= q_pos[:, None]).astype(jnp.int32), axis=1)
    last_local = jnp.clip(group_end - 1 - my_start, 0, shard_rows - 1)
    present = (group_start < my_start + shard_rows) & (group_end > my_start)
    q_piece = lax.all_gather(queries, "seq", axis=0, tiled=True)
    count = q_piece.shape[0]
    q_rows = q_piece.reshape(count * q_piece.shape[1], q_piece.shape[2])
    similar = jnp.einsum("td,rd->tr", q_rows, embedded, preferred_element_type=jnp.float32)
    running = segmented_max(similar, group_id)
    picked = jnp.take(running, last_local, axis=1)
    picked = jnp.where(present[None, :], picked, -jnp.inf)
    part_max = picked.reshape(count, q_piece.shape[1], picked.shape[-1])
    own_count = queries.shape[0]
    all_maxima = lax.pmax(part_max, "seq")
    token_max = lax.dynamic_slice_in_dim(all_maxima, seq_place * own_count, own_count, 0)
    live_mask = (jnp.arange(LQ, dtype=jnp.int32)[None, :] < query_lengths[:, None]).astype(
        jnp.float32
    )
    scores = (
        jnp.sum(token_max * live_mask[:, :, None], axis=1)
        / query_lengths.astype(jnp.float32)[:, None]
    )
    student_scores = scores / SOFTMAX_TEMP
    student_scores = student_scores - jnp.max(student_scores, axis=-1, keepdims=True)
    student_log_prob = student_scores - jnp.log(
        jnp.sum(jnp.exp(student_scores), axis=-1, keepdims=True)
    )
    target_scores = teacher / SOFTMAX_TEMP
    target_scores = target_scores - jnp.max(target_scores, axis=-1, keepdims=True)
    log_t = target_scores - jnp.log(jnp.sum(jnp.exp(target_scores), axis=-1, keepdims=True))
    teacher_prob = jnp.exp(log_t)
    kl_terms = jnp.sum(teacher_prob * (log_t - student_log_prob), axis=-1)
    query_count_all = own_count * seq_count * lax.axis_size("pb")
    distill_loss = lax.psum(jnp.sum(kl_terms), ("seq", "pb")) / query_count_all
    score_gradient = (jnp.exp(student_log_prob) - teacher_prob) / (SOFTMAX_TEMP * query_count_all)
    return (embedded, scores, score_gradient, distill_loss)


def solution(mesh):
    placed = (
        P("seq", None),
        P(None, "pb"),
        P(None, "pb"),
        P(None, "pb"),
        P("pb", None),
        P(),
        P(),
        P(("seq", "pb"), None, None),
        P(("seq", "pb")),
        P(),
        P(("seq", "pb"), None),
    )
    return jax.shard_map(
        per_device,
        mesh=mesh,
        in_specs=placed,
        out_specs=(P("seq", None), P(("seq", "pb"), None), P(("seq", "pb"), None), P()),
        check_vma=False,
    )
```

profile of v0, /device:TPU:2, one launch (start us, length us, event | category | flops | bytes accessed | tf_op | source)
XLA Modules:
  0.0 510.9 jit_solution(6274992664846566963)
XLA Ops:
  8.1 1.6 fusion.10
  9.8 2.8 fusion.15
  12.6 0.7 fusion.14
  13.4 0.7 copy-done.5
  14.1 0.8 pad_maximum_fusion
  14.9 6.0 %collective-permute-start = (bf16[2,256,512]{2,1,0:T(8,128)(2,1)}, bf16[2,256,512]{2,1,0:T(8,128)(2,1)}, u32[]{:S(2)}, u32[]{:S(2)}) collective-permute-start(bf16[2,256,512]{2,1,0:T(8,128)(2,1)} %pad_maximum_fusion), channel_id=1, source_target_pairs={{0,16},{4,20},{8,24},{12,28},{16,32},{20,36},{24,40},{28,44},{32,4... | collective-permute-start | bytes 1572872 | tf_op jit(solution)/shard_map/ppermute | solution.py:18
  20.9 3.8 collective-permute-start.1
  24.7 5.0 collective-permute-start.2
  29.7 3.0 collective-permute-start.3
  32.8 1.3 collective-permute-start.4
  34.1 1.7 fusion.9
  35.8 3.0 fusion.16
  38.8 1.4 collective-permute-start.5
  40.3 1.1 constant_dynamic-update-slice_fusion.8
  41.3 18.7 %collective-permute-done.1 = bf16[2,256,512]{2,1,0:T(8,128)(2,1)} collective-permute-done((bf16[2,256,512]{2,1,0:T(8,128)(2,1)}, bf16[2,256,512]{2,1,0:T(8,128)(2,1)}, u32[]{:S(2)}, u32[]{:S(2)}) %collective-permute-start.1) | collective-permute-done | bytes 524320 | tf_op jit(solution)/shard_map/ppermute | solution.py:18
  60.0 1.3 collective-permute-start.6
  61.3 1.1 constant_dynamic-update-slice_fusion.7
  62.4 9.7 %collective-permute-done.2 = bf16[2,256,512]{2,1,0:T(8,128)(2,1)} collective-permute-done((bf16[2,256,512]{2,1,0:T(8,128)(2,1)}, bf16[2,256,512]{2,1,0:T(8,128)(2,1)}, u32[]{:S(2)}, u32[]{:S(2)}) %collective-permute-start.2) | collective-permute-done | bytes 524320 | tf_op jit(solution)/shard_map/ppermute | solution.py:18
  72.1 1.3 collective-permute-start.7
  73.4 1.1 constant_dynamic-update-slice_fusion.6
  74.5 1.1 constant_dynamic-update-slice_fusion.5
  75.7 1.1 constant_dynamic-update-slice_fusion.3
  76.9 29.0 %collective-permute-done.7 = bf16[2,256,512]{2,1,0:T(8,128)(2,1)S(1)} collective-permute-done((bf16[2,256,512]{2,1,0:T(8,128)(2,1)}, bf16[2,256,512]{2,1,0:T(8,128)(2,1)S(1)}, u32[]{:S(2)}, u32[]{:S(2)}) %collective-permute-start.7) | collective-permute-done | bytes 524320 | tf_op jit(solution)/shard_map/ppermute | solution.py:18
  105.9 2.4 fusion.39
  108.4 4.3 copy.34
  112.7 5.3 %reshape_squeeze.7 = bf16[2304,4,128]{2,1,0:T(4,128)(2,1)} reshape(bf16[1,2304,512]{2,1,0:T(8,128)(2,1)} %get-tuple-element.8) | data formatting | bytes 4718592 | tf_op jit(solution)/shard_map/reshape;squeeze | solution.py:78
  118.0 8.8 %fusion.40 = (f32[4,256]{1,0:T(4,128)S(1)}, f32[4,256,2304]{2,1,0:T(8,128)}) fusion(pred[256,2304]{1,0:T(8,128)(4,1)} %fusion.9, bf16[2304,4,128]{2,1,0:T(4,128)(2,1)} %reshape_squeeze.7, bf16[32,4,8,128]{3,2,1,0:T(8,128)(2,1)S(1)} %copy-done.13), kind=kOutput, calls=%fused_computation.89 | convolution fusion | flops 613419264 | bytes 12652544 | tf_op jit(solution)/shard_map/sub | solution.py:85
  126.8 6.2 %fusion.13 = bf16[4,128,256]{2,1,0:T(8,128)(2,1)S(1)} fusion(bf16[2304,4,128]{0,2,1:T(8,128)(2,1)} %bitcast.54, f32[4,256,2304]{2,1,0:T(8,128)} %get-tuple-element.23, f32[4,256]{1,0:T(4,128)S(1)} %get-tuple-element.22), kind=kOutput, calls=%fused_computation.32 | convolution fusion | flops 608829440 | bytes 12062720 | tf_op jit(solution)/shard_map/hqk,khd->qhd/dot_general | solution.py:87
  133.0 2.0 fusion.45
  135.1 0.5 all-gather.2.cloned.1.call-update
  135.6 0.2 all-reduce.20.cloned.1.call-start
  135.9 0.1 copy.32
  136.0 0.2 reduce-window.4
  136.1 0.1 fusion.31
  136.3 0.2 convert_reduce_fusion
  136.6 63.6 %all-reduce.18.cloned.1.call-done = f32[256,2048]{1,0:T(8,128)} async-done(((f32[256,2048]{1,0:T(8,128)}), f32[256,2048]{1,0:T(8,128)}) %all-reduce.18.cloned.1.call-update) | async-done | bytes 2097168 | tf_op jit(solution)/shard_map/psum | solution.py:90
  200.2 2.1 multiply_reduce_fusion
  202.3 0.1 copy-done.3
  202.4 0.4 multiply_convert_fusion
  202.8 20.9 %all-gather.2.cloned.1.call-done = bf16[64,32,2048]{2,1,0:T(8,128)(2,1)} async-done(((bf16[1,32,2048]{2,1,0:T(8,128)(2,1)}), bf16[64,32,2048]{2,1,0:T(8,128)(2,1)}) %all-gather.2.cloned.1.call-update) | async-done | bytes 8388624 | tf_op jit(solution)/shard_map/all_gather | solution.py:97
  223.7 5.7 %convolution_bitcast_fusion = f32[2048,256]{0,1:T(8,128)S(1)} fusion(bf16[256,2048]{1,0:T(8,128)(2,1)S(1)} %multiply_convert_fusion, bf16[2048,2048]{1,0:T(8,128)(2,1)} %bitcast.65), kind=kOutput, calls=%fused_computation.21 | convolution fusion | flops 2147483648 | bytes 11534336 | tf_op jit(solution)/shard_map/td,rd->tr/dot_general | solution.py:100
  229.5 0.3 maximum_select_fusion.7
  229.8 0.4 maximum_select_fusion.6
  230.2 0.4 maximum_select_fusion.5
  230.5 0.2 slice.79
  230.7 0.3 maximum_select_fusion.4
  231.1 0.2 slice.80
  231.3 0.3 maximum_select_fusion.3
  231.6 0.2 slice.81
  231.8 0.3 maximum_select_fusion.2
  232.1 0.1 slice.82
  232.2 0.3 maximum_select_fusion.1
  232.7 0.3 maximum_select_fusion
  233.0 1.0 gather_fusion
  234.0 1.4 copy.33
  235.3 2.4 select_select_fusion
  238.4 0.6 multiply_reduce_fusion.3
  239.0 1.2 exponential_reduce_fusion
  240.9 180.9 %all-reduce.20.cloned.1.call-done = f32[64,32,128]{2,1,0:T(8,128)} async-done(((f32[64,32,128]{2,1,0:T(8,128)}), f32[64,32,128]{2,1,0:T(8,128)}) %all-reduce.20.cloned.1.call-update) | async-done | bytes 1048592 | tf_op jit(solution)/shard_map/pmax | solution.py:106
  421.8 0.8 multiply_reduce_fusion.1
  422.6 0.6 multiply_reduce_fusion.4
  423.2 1.3 exponential_reduce_fusion.1
  425.1 2.5 multiply_reduce_fusion.2
  427.6 74.0 %psum.15 = f32[]{:T(128)} all-reduce(f32[]{:T(128)} %get-tuple-element.10), channel_id=1, replica_groups=mesh['seq'=64,'pb'=4] {'seq','pb'}, use_global_device_ids=true, to_apply=%region_14.15 | all-reduce | flops 1 | bytes 8 | tf_op jit(solution)/shard_map/psum | solution.py:126
  (50 shorter events, 0.6 us)
Async XLA Ops:
  8.0 125.0 %copy-start = (bf16[512,2048]{1,0:T(8,128)(2,1)S(1)}, bf16[512,2048]{1,0:T(8,128)(2,1)}, u32[]{:S(2)}) copy-start(bf16[512,2048]{1,0:T(8,128)(2,1)} %param.15) | copy-start | bytes 6291460
  8.0 192.1 %all-reduce.18.cloned.1.call-start = ((), (), s32[]{:S(2)}) async-start(), calls=%async_computation | async-start | bytes 4194304 | tf_op jit(solution)/shard_map/psum | solution.py:90
  9.7 2.9 copy-start.2
  9.7 2.9 copy-start.11
  9.7 2.9 copy-start.12
  13.4 0.7 copy-start.5
  14.9 23.9 %collective-permute-start = (bf16[2,256,512]{2,1,0:T(8,128)(2,1)}, bf16[2,256,512]{2,1,0:T(8,128)(2,1)}, u32[]{:S(2)}, u32[]{:S(2)}) collective-permute-start(bf16[2,256,512]{2,1,0:T(8,128)(2,1)} %pad_maximum_fusion), channel_id=1, source_target_pairs={{0,16},{4,20},{8,24},{12,28},{16,32},{20,36},{24,40},{28,44},{32,4... | collective-permute-start | bytes 1572872 | tf_op jit(solution)/shard_map/ppermute | solution.py:18
  20.9 39.1 %collective-permute-start.1 = (bf16[2,256,512]{2,1,0:T(8,128)(2,1)}, bf16[2,256,512]{2,1,0:T(8,128)(2,1)}, u32[]{:S(2)}, u32[]{:S(2)}) collective-permute-start(bf16[2,256,512]{2,1,0:T(8,128)(2,1)} %pad_maximum_fusion), channel_id=1, source_target_pairs={{0,12},{4,16},{8,20},{12,24},{16,28},{20,32},{24,36},{28,40},{32,4... | collective-permute-start | bytes 1572872 | tf_op jit(solution)/shard_map/ppermute | solution.py:18
  24.7 47.4 %collective-permute-start.2 = (bf16[2,256,512]{2,1,0:T(8,128)(2,1)}, bf16[2,256,512]{2,1,0:T(8,128)(2,1)}, u32[]{:S(2)}, u32[]{:S(2)}) collective-permute-start(bf16[2,256,512]{2,1,0:T(8,128)(2,1)} %pad_maximum_fusion), channel_id=1, source_target_pairs={{0,8},{4,12},{8,16},{12,20},{16,24},{20,28},{24,32},{28,36},{32,40... | collective-permute-start | bytes 1572872 | tf_op jit(solution)/shard_map/ppermute | solution.py:18
  29.7 44.8 %collective-permute-start.3 = (bf16[2,256,512]{2,1,0:T(8,128)(2,1)}, bf16[2,256,512]{2,1,0:T(8,128)(2,1)}, u32[]{:S(2)}, u32[]{:S(2)}) collective-permute-start(bf16[2,256,512]{2,1,0:T(8,128)(2,1)} %pad_maximum_fusion), channel_id=1, source_target_pairs={{0,4},{4,8},{8,12},{12,16},{16,20},{20,24},{24,28},{28,32},{32,36}... | collective-permute-start | bytes 1572872 | tf_op jit(solution)/shard_map/ppermute | solution.py:18
  32.8 42.9 %collective-permute-start.4 = (bf16[2,256,512]{2,1,0:T(8,128)(2,1)}, bf16[2,256,512]{2,1,0:T(8,128)(2,1)}, u32[]{:S(2)}, u32[]{:S(2)}) collective-permute-start(bf16[2,256,512]{2,1,0:T(8,128)(2,1)} %pad_maximum_fusion), channel_id=1, source_target_pairs={{4,0},{8,4},{12,8},{16,12},{20,16},{24,20},{28,24},{32,28},{36,32}... | collective-permute-start | bytes 1572872 | tf_op jit(solution)/shard_map/ppermute | solution.py:18
  38.8 36.8 %copy-start.6 = (bf16[1,256,512]{2,1,0:T(8,128)(2,1)S(1)}, bf16[1,256,512]{2,1,0:T(8,128)(2,1)}, u32[]{:S(2)}) copy-start(bf16[1,256,512]{2,1,0:T(8,128)(2,1)} %copy-done.5) | copy-start | bytes 786436
  38.8 37.9 %collective-permute-start.5 = (bf16[2,256,512]{2,1,0:T(8,128)(2,1)}, bf16[2,256,512]{2,1,0:T(8,128)(2,1)S(1)}, u32[]{:S(2)}, u32[]{:S(2)}) collective-permute-start(bf16[2,256,512]{2,1,0:T(8,128)(2,1)} %pad_maximum_fusion), channel_id=1, source_target_pairs={{8,0},{12,4},{16,8},{20,12},{24,16},{28,20},{32,24},{36,28},{40,32... | collective-permute-start | bytes 1572872 | tf_op jit(solution)/shard_map/ppermute | solution.py:18
  60.0 16.8 %collective-permute-start.6 = (bf16[2,256,512]{2,1,0:T(8,128)(2,1)}, bf16[2,256,512]{2,1,0:T(8,128)(2,1)S(1)}, u32[]{:S(2)}, u32[]{:S(2)}) collective-permute-start(bf16[2,256,512]{2,1,0:T(8,128)(2,1)} %pad_maximum_fusion), channel_id=1, source_target_pairs={{12,0},{16,4},{20,8},{24,12},{28,16},{32,20},{36,24},{40,28},{44,3... | collective-permute-start | bytes 1572872 | tf_op jit(solution)/shard_map/ppermute | solution.py:18
  72.1 33.7 %collective-permute-start.7 = (bf16[2,256,512]{2,1,0:T(8,128)(2,1)}, bf16[2,256,512]{2,1,0:T(8,128)(2,1)S(1)}, u32[]{:S(2)}, u32[]{:S(2)}) collective-permute-start(bf16[2,256,512]{2,1,0:T(8,128)(2,1)} %pad_maximum_fusion), channel_id=1, source_target_pairs={{16,0},{20,4},{24,8},{28,12},{32,16},{36,20},{40,24},{44,28},{48,3... | collective-permute-start | bytes 1572872 | tf_op jit(solution)/shard_map/ppermute | solution.py:18
  112.7 5.3 %copy-start.13 = (bf16[32,4,8,128]{3,2,1,0:T(8,128)(2,1)S(1)}, bf16[32,4,8,128]{3,2,1,0:T(8,128)(2,1)}, u32[]{:S(2)}) copy-start(bf16[32,4,8,128]{3,2,1,0:T(8,128)(2,1)} %fusion.16) | copy-start | bytes 786436
  135.0 0.8 copy-start.8
  135.0 67.3 %copy-start.7 = (f32[2048]{0:T(1024)S(1)}, f32[2048]{0:T(1024)}, u32[]{:S(2)}) copy-start(f32[2048]{0:T(1024)} %param.17) | copy-start | bytes 24580
  135.0 88.7 %all-gather.2.cloned.1.call-start = ((), (), s32[]{:S(2)}) async-start(), calls=%async_computation.1 | async-start | bytes 8519680 | tf_op jit(solution)/shard_map/all_gather | solution.py:97
  135.6 286.2 %all-reduce.20.cloned.1.call-start = ((), (), s32[]{:S(2)}) async-start(), calls=%async_computation.2 | async-start | bytes 2097152 | tf_op jit(solution)/shard_map/pmax | solution.py:106
  200.2 2.3 copy-start.3
  202.8 26.7 %copy-start.4 = (bf16[256,2048]{1,0:T(8,128)(2,1)}, bf16[256,2048]{1,0:T(8,128)(2,1)S(1)}, u32[]{:S(2)}) copy-start(bf16[256,2048]{1,0:T(8,128)(2,1)S(1)} %multiply_convert_fusion) | copy-start | bytes 3145732
  234.0 268.3 %copy-start.1 = (bf16[512,2048]{1,0:T(8,128)(2,1)S(1)}, bf16[512,2048]{1,0:T(8,128)(2,1)}, u32[]{:S(2)}) copy-start(bf16[512,2048]{1,0:T(8,128)(2,1)} %param.15) | copy-start | bytes 6291460
  235.3 3.0 copy-start.10
  423.2 79.1 %copy-start.9 = (f32[128]{0:T(128)}, f32[128]{0:T(128)S(1)}, u32[]{:S(2)}) copy-start(f32[128]{0:T(128)S(1)} %get-tuple-element.7) | copy-start | bytes 1540
Sparse Core Ops, SparseCore 0:
  135.1 64.9 all-reduce.17
Sparse Core Ops, SparseCore 1:
  138.3 85.4 all-gather.1
  237.8 183.9 all-reduce.19
where the time goes:
time: 514 us; the launch traced here: 511 us
  waiting for transfers between devices  323 us (63%)
  blocking collectives  74 us (14%)
  matrix products  29.3 us (6%)
  starting transfers between devices  23.4 us (5%)
  local copies, waits for them, and re-layouts  21.8 us (4%)
  between operations  19.8 us (4%)
  other arithmetic  19.2 us (4%)
    pmax x1, waiting for transfers between devices, per_device(): all_maxima = lax.pmax(part_max, 'seq')  181 us
    psum x1, blocking collectives, per_device(): distill_loss = lax.psum(jnp.sum(kl_terms), ('seq', 'pb')) / query_count_all  74 us
    psum x1, waiting for transfers between devices, per_device(): attn_sum = lax.psum(partial_value, 'pb')  63.6 us
    ppermute x8, waiting for transfers between devices, shifted_2(): return lax.ppermute(x, axis, pairs)  57.5 us
    ppermute x8, starting transfers between devices, shifted_2(): return lax.ppermute(x, axis, pairs)  23.1 us
    all_gather x1, waiting for transfers between devices, per_device(): q_piece = lax.all_gather(queries, 'seq', axis=0, tiled=True)  20.9 us
  transfers between devices with their start and end apart: 11, of which 6 were waited for; matrix products, arithmetic and copies ran while one was open for 3% of the time, Pallas kernels for 0%

commit v1 on v0

--- a/solution.py
+++ b/solution.py
@@ -16,6 +16,45 @@
     count = lax.axis_size(axis)
     pairs = [(i, i + by) for i in range(count) if 0 <= i + by < count]
     return lax.ppermute(x, axis, pairs)
+
+
+def xor_swap(x, axis, bit):
+    count = lax.axis_size(axis)
+    return lax.ppermute(x, axis, [(i, i ^ bit) for i in range(count)])
+
+
+def ring_shift(x, axis, by):
+    count = lax.axis_size(axis)
+    return lax.ppermute(x, axis, [(i, (i + by) % count) for i in range(count)])
+
+
+HALVING_BITS = (1, 2, 16, 4, 32, 8)
+
+
+def halving_max(values, axis):
+    place = lax.axis_index(axis)
+    rows = values.shape[0]
+    width = rows.bit_length() - 1
+    bits = [b for b in HALVING_BITS if b < rows]
+    split = values.reshape((2,) * width + values.shape[1:])
+    order = [width - 1 - (b.bit_length() - 1) for b in bits]
+    split = jnp.transpose(split, order + list(range(width, split.ndim)))
+    values = split.reshape((rows,) + values.shape[1:])
+    for bit in bits:
+        half = values.shape[0] // 2
+        mine = ((place & bit) != 0).astype(jnp.int32)
+        keep = lax.dynamic_slice_in_dim(values, mine * half, half, 0)
+        send = lax.dynamic_slice_in_dim(values, (1 - mine) * half, half, 0)
+        values = jnp.maximum(keep, xor_swap(send, axis, bit))
+    return values
+
+
+def butterfly_sum(value, axis):
+    count = lax.axis_size(axis)
+    bits = [b for b in HALVING_BITS if b < count]
+    for bit in bits:
+        value = value + xor_swap(value, axis, bit)
+    return value
 
 
 def rms_scale(values, gain):
@@ -86,8 +125,14 @@
     weights = (exp_terms / jnp.sum(exp_terms, axis=-1, keepdims=True)).astype(jnp.bfloat16)
     mixed = jnp.einsum("hqk,khd->qhd", weights, v_heads, preferred_element_type=jnp.float32)
     mixed = mixed.reshape(shard_rows, head_width).astype(jnp.bfloat16)
-    partial_value = jnp.dot(mixed, w_out, preferred_element_type=jnp.float32)
-    attn_sum = lax.psum(partial_value, "pb")
+    pb_count = lax.axis_size("pb")
+    mixed_parts = [mixed] + [ring_shift(mixed, "pb", k) for k in range(1, pb_count)]
+    w_out_parts = [w_out] + [ring_shift(w_out, "pb", k) for k in range(1, pb_count)]
+    attn_sum = jnp.dot(
+        jnp.concatenate(mixed_parts, axis=1),
+        jnp.concatenate(w_out_parts, axis=0),
+        preferred_element_type=jnp.float32,
+    )
     embedded = rms_scale(residual + attn_sum, gain_embed).astype(jnp.bfloat16)
     group_end = jnp.cumsum(group_lengths)
     group_start = group_end - group_lengths
@@ -103,8 +148,7 @@
     picked = jnp.where(present[None, :], picked, -jnp.inf)
     part_max = picked.reshape(count, q_piece.shape[1], picked.shape[-1])
     own_count = queries.shape[0]
-    all_maxima = lax.pmax(part_max, "seq")
-    token_max = lax.dynamic_slice_in_dim(all_maxima, seq_place * own_count, own_count, 0)
+    token_max = halving_max(part_max, "seq")
     live_mask = (jnp.arange(LQ, dtype=jnp.int32)[None, :] < query_lengths[:, None]).astype(
         jnp.float32
     )
@@ -123,7 +167,8 @@
     teacher_prob = jnp.exp(log_t)
     kl_terms = jnp.sum(teacher_prob * (log_t - student_log_prob), axis=-1)
     query_count_all = own_count * seq_count * lax.axis_size("pb")
-    distill_loss = lax.psum(jnp.sum(kl_terms), ("seq", "pb")) / query_count_all
+    loss_sum = butterfly_sum(butterfly_sum(jnp.sum(kl_terms), "seq"), "pb")
+    distill_loss = loss_sum / query_count_all
     score_gradient = (jnp.exp(student_log_prob) - teacher_prob) / (SOFTMAX_TEMP * query_count_all)
     return (embedded, scores, score_gradient, distill_loss)
 

time: 514 us -> 311 us (0.61)
  waiting for transfers between devices: 323 us -> 147 us
  blocking collectives: 74 us -> 0 us
  starting transfers between devices: 23.4 us -> 73.5 us
    pmax x1 -> x0, waiting for transfers between devices: 181 us -> none  [per_device(): all_maxima = lax.pmax(part_max, 'seq')]
    psum x1 -> x0, blocking collectives: 74 us -> none  [per_device(): distill_loss = lax.psum(jnp.sum(kl_terms), ('seq', 'pb')) / query_count_all]
    ppermute x0 -> x20, waiting for transfers between devices: none -> 68.1 us  [the longest x6 37.3 us: ring_shift(): return lax.ppermute(x, axis, [(i, (i + by) % count) for i in range(count)])]
    psum x1 -> x0, waiting for transfers between devices: 63.6 us -> none  [per_device(): attn_sum = lax.psum(partial_value, 'pb')]
    ppermute x0 -> x20, starting transfers between devices: none -> 51.2 us  [the longest x14 42.4 us: xor_swap(): return lax.ppermute(x, axis, [(i, i ^ bit) for i in range(count)])]
    ppermute x8, waiting for transfers between devices: 57.5 us -> 78.7 us  [shifted_2(): return lax.ppermute(x, axis, pairs)]
    all_gather x1, waiting for transfers between devices: 20.9 us -> 0.02 us  [per_device(): q_piece = lax.all_gather(queries, 'seq', axis=0, tiled=True)]
  transfers between devices with their start and end apart: 11 -> 29, of which waited for: 6 -> 19; matrix products, arithmetic and copies ran while one was open for 3% -> 14% of each run, Pallas kernels for 0% -> 0%
where the time goes in v1:
time: 311 us; the launch traced here: 310 us
  waiting for transfers between devices  147 us (47%)
  starting transfers between devices  73.5 us (24%)
  matrix products  32 us (10%)
  between operations  23.8 us (8%)
  local copies, waits for them, and re-layouts  17.3 us (6%)
  other arithmetic  16.1 us (5%)
    ppermute x8, waiting for transfers between devices, shifted_2(): return lax.ppermute(x, axis, pairs)  78.7 us
    ppermute x14, starting transfers between devices, xor_swap(): return lax.ppermute(x, axis, [(i, i ^ bit) for i in range(count)])  42.4 us
    ppermute x6, waiting for transfers between devices, ring_shift(): return lax.ppermute(x, axis, [(i, (i + by) % count) for i in range(count)])  37.3 us
    ppermute x14, waiting for transfers between devices, xor_swap(): return lax.ppermute(x, axis, [(i, i ^ bit) for i in range(count)])  30.8 us
    ppermute x8, starting transfers between devices, shifted_2(): return lax.ppermute(x, axis, pairs)  22.2 us
    sub x1, matrix products, per_device(): exp_terms = jnp.exp(logits - row_max)  8.86 us
    ppermute x6, starting transfers between devices, ring_shift(): return lax.ppermute(x, axis, [(i, (i + by) % count) for i in range(count)])  8.85 us
  transfers between devices with their start and end apart: 29, of which 19 were waited for; matrix products, arithmetic and copies ran while one was open for 14% of the time, Pallas kernels for 0%

profile of v1, /device:TPU:2, one launch (start us, length us, event | category | flops | bytes accessed | tf_op | source)
XLA Modules:
  0.0 310.2 jit_solution(16918581950994711516)
XLA Ops:
  7.9 1.5 fusion.20
  9.5 2.1 fusion.24
  12.5 6.0 %collective-permute-start = (bf16[2,256,512]{2,1,0:T(8,128)(2,1)S(1)}, bf16[2,256,512]{2,1,0:T(8,128)(2,1)}, u32[]{:S(2)}, u32[]{:S(2)}) collective-permute-start(bf16[2,256,512]{2,1,0:T(8,128)(2,1)S(1)} %pad_maximum_fusion), channel_id=1, source_target_pairs={{0,16},{4,20},{8,24},{12,28},{16,32},{20,36},{24,40},{28,44},{32,4... | collective-permute-start | bytes 1572872 | tf_op jit(solution)/shard_map/ppermute | solution.py:18
  18.5 3.8 %collective-permute-start.1 = (bf16[2,256,512]{2,1,0:T(8,128)(2,1)S(1)}, bf16[2,256,512]{2,1,0:T(8,128)(2,1)}, u32[]{:S(2)}, u32[]{:S(2)}) collective-permute-start(bf16[2,256,512]{2,1,0:T(8,128)(2,1)S(1)} %pad_maximum_fusion), channel_id=1, source_target_pairs={{0,12},{4,16},{8,20},{12,24},{16,28},{20,32},{24,36},{28,40},{32,4... | collective-permute-start | bytes 1572872 | tf_op jit(solution)/shard_map/ppermute | solution.py:18
  22.3 5.0 %collective-permute-start.2 = (bf16[2,256,512]{2,1,0:T(8,128)(2,1)S(1)}, bf16[2,256,512]{2,1,0:T(8,128)(2,1)}, u32[]{:S(2)}, u32[]{:S(2)}) collective-permute-start(bf16[2,256,512]{2,1,0:T(8,128)(2,1)S(1)} %pad_maximum_fusion), channel_id=1, source_target_pairs={{0,8},{4,12},{8,16},{12,20},{16,24},{20,28},{24,32},{28,36},{32,40... | collective-permute-start | bytes 1572872 | tf_op jit(solution)/shard_map/ppermute | solution.py:18
  27.3 2.3 collective-permute-start.3
  29.6 1.3 collective-permute-start.4
  31.0 1.7 fusion.19
  32.6 3.1 fusion.26
  36.1 1.3 collective-permute-start.5
  37.4 1.1 constant_dynamic-update-slice_fusion.8
  38.5 23.7 %collective-permute-done.1 = bf16[2,256,512]{2,1,0:T(8,128)(2,1)} collective-permute-done((bf16[2,256,512]{2,1,0:T(8,128)(2,1)S(1)}, bf16[2,256,512]{2,1,0:T(8,128)(2,1)}, u32[]{:S(2)}, u32[]{:S(2)}) %collective-permute-start.1) | collective-permute-done | bytes 524320 | tf_op jit(solution)/shard_map/ppermute | solution.py:18
  62.2 1.3 collective-permute-start.6
  63.5 1.1 constant_dynamic-update-slice_fusion.7
  64.6 14.2 %collective-permute-done.2 = bf16[2,256,512]{2,1,0:T(8,128)(2,1)} collective-permute-done((bf16[2,256,512]{2,1,0:T(8,128)(2,1)S(1)}, bf16[2,256,512]{2,1,0:T(8,128)(2,1)}, u32[]{:S(2)}, u32[]{:S(2)}) %collective-permute-start.2) | collective-permute-done | bytes 524320 | tf_op jit(solution)/shard_map/ppermute | solution.py:18
  78.8 1.3 collective-permute-start.7
  80.1 1.1 constant_dynamic-update-slice_fusion.6
  81.2 1.6 collective-permute-start.11
  82.8 1.2 collective-permute-start.12
  84.1 2.6 collective-permute-start.13
  86.7 40.8 %collective-permute-done.7 = bf16[2,256,512]{2,1,0:T(8,128)(2,1)S(1)} collective-permute-done((bf16[2,256,512]{2,1,0:T(8,128)(2,1)S(1)}, bf16[2,256,512]{2,1,0:T(8,128)(2,1)S(1)}, u32[]{:S(2)}, u32[]{:S(2)}) %collective-permute-start.7) | collective-permute-done | bytes 524320 | tf_op jit(solution)/shard_map/ppermute | solution.py:18
  127.6 1.7 fusion.57
  129.3 5.3 %reshape_squeeze.7 = bf16[2304,4,128]{2,1,0:T(4,128)(2,1)} reshape(bf16[1,2304,512]{2,1,0:T(8,128)(2,1)} %get-tuple-element.8) | data formatting | bytes 4718592 | tf_op jit(solution)/shard_map/reshape;squeeze | solution.py:117
  134.6 8.9 %fusion.58 = (f32[4,256]{1,0:T(4,128)S(1)}, f32[4,256,2304]{2,1,0:T(8,128)}) fusion(pred[256,2304]{1,0:T(8,128)(4,1)} %fusion.19, bf16[2304,4,128]{2,1,0:T(4,128)(2,1)} %reshape_squeeze.7, bf16[32,4,8,128]{3,2,1,0:T(8,128)(2,1)} %fusion.26), kind=kOutput, calls=%fused_computation.116 | convolution fusion | flops 613419264 | bytes 12652544 | tf_op jit(solution)/shard_map/sub | solution.py:124
  143.4 2.5 copy.37
  146.0 6.1 %fusion.23 = bf16[4,128,256]{2,1,0:T(8,128)(2,1)S(1)} fusion(bf16[2304,4,128]{0,2,1:T(8,128)(2,1)} %bitcast.57, f32[4,256,2304]{2,1,0:T(8,128)} %get-tuple-element.23, f32[4,256]{1,0:T(4,128)S(1)} %get-tuple-element.22), kind=kOutput, calls=%fused_computation.40 | convolution fusion | flops 608829440 | bytes 12062720 | tf_op jit(solution)/shard_map/hqk,khd->qhd/dot_general | solution.py:126
  153.0 1.5 collective-permute-start.8
  154.5 28.9 %collective-permute-done.10 = bf16[256,512]{0,1:T(8,128)(2,1)S(1)} collective-permute-done((bf16[256,512]{0,1:T(8,128)(2,1)S(1)}, bf16[256,512]{0,1:T(8,128)(2,1)S(1)}, u32[]{:S(2)}, u32[]{:S(2)}) %collective-permute-start.10) | collective-permute-done | bytes 262176 | tf_op jit(solution)/shard_map/ppermute | solution.py:28
  183.4 1.3 collective-permute-start.9
  184.8 8.4 %collective-permute-done.9 = bf16[256,512]{0,1:T(8,128)(2,1)S(1)} collective-permute-done((bf16[256,512]{0,1:T(8,128)(2,1)S(1)}, bf16[256,512]{0,1:T(8,128)(2,1)S(1)}, u32[]{:S(2)}, u32[]{:S(2)}) %collective-permute-start.9) | collective-permute-done | bytes 262176 | tf_op jit(solution)/shard_map/ppermute | solution.py:28
  193.2 5.0 %multiply_reduce_fusion = (f32[256]{0:T(256)S(1)}, f32[256,2048]{1,0:T(8,128)S(1)}) fusion(bf16[512,2048]{1,0:T(8,128)(2,1)} %collective-permute-done.13, bf16[512,2048]{1,0:T(8,128)(2,1)} %collective-permute-done.12, bf16[512,2048]{1,0:T(8,128)(2,1)} %collective-permute-done.11, bf16[512,2048]{1,0:T(8,128)(2,1)} %param.15, ...), kind=kOutput, calls=%fused_computation.39 | convolution fusion | flops 2187329280 | bytes 12583936 | tf_op jit(solution)/shard_map/dot_general | solution.py:131
  198.5 6.1 %convolution_bitcast_fusion = f32[2048,256]{0,1:T(8,128)S(1)} fusion(bf16[256,2048]{1,0:T(8,128)(2,1)S(1)} %multiply_convert_fusion, bf16[2048,2048]{1,0:T(8,128)(2,1)} %bitcast.67), kind=kOutput, calls=%fused_computation.29 | convolution fusion | flops 2147483648 | bytes 11534336 | tf_op jit(solution)/shard_map/td,rd->tr/dot_general | solution.py:145
  208.1 1.0 gather_fusion
  210.6 2.2 collective-permute-done.14
  212.8 1.9 dynamic-slice_maximum_fusion
  214.7 1.0 constant_dynamic-slice_fusion.4
  215.7 6.5 %collective-permute-start.15 = (f32[16,32,128]{2,1,0:T(8,128)S(1)}, f32[16,32,128]{2,1,0:T(8,128)S(1)}, u32[]{:S(2)}, u32[]{:S(2)}) collective-permute-start(f32[16,32,128]{2,1,0:T(8,128)S(1)} %constant_dynamic-slice_fusion.4), channel_id=1, source_target_pairs={{0,8},{4,12},{8,0},{12,4},{16,24},{20,28},{24,16},{28,20},{32,40},... | collective-permute-start | bytes 786440 | tf_op jit(solution)/shard_map/ppermute | solution.py:23
  222.2 6.6 %collective-permute-done.15 = f32[16,32,128]{2,1,0:T(8,128)S(1)} collective-permute-done((f32[16,32,128]{2,1,0:T(8,128)S(1)}, f32[16,32,128]{2,1,0:T(8,128)S(1)}, u32[]{:S(2)}, u32[]{:S(2)}) %collective-permute-start.15) | collective-permute-done | bytes 262176 | tf_op jit(solution)/shard_map/ppermute | solution.py:23
  228.8 1.0 dynamic-slice_maximum_fusion.1
  229.8 1.1 collective-permute-start.16
  230.9 4.0 %collective-permute-done.16 = f32[8,32,128]{2,1,0:T(8,128)S(1)} collective-permute-done((f32[8,32,128]{2,1,0:T(8,128)S(1)}, f32[8,32,128]{2,1,0:T(8,128)S(1)}, u32[]{:S(2)}, u32[]{:S(2)}) %collective-permute-start.16) | collective-permute-done | bytes 131104 | tf_op jit(solution)/shard_map/ppermute | solution.py:23
  234.9 5.5 %collective-permute-start.17 = (f32[4,32,128]{2,1,0:T(8,128)S(1)}, f32[4,32,128]{2,1,0:T(8,128)S(1)}, u32[]{:S(2)}, u32[]{:S(2)}) collective-permute-start(f32[4,32,128]{2,1,0:T(8,128)S(1)} %constant_dynamic-slice_fusion.2), channel_id=1, source_target_pairs={{0,16},{4,20},{8,24},{12,28},{16,0},{20,4},{24,8},{28,12},{32,48},... | collective-permute-start | bytes 196616 | tf_op jit(solution)/shard_map/ppermute | solution.py:23
  241.0 2.1 collective-permute-done.17
  243.2 2.8 collective-permute-start.18
  246.0 1.2 exponential_reduce_fusion
  247.8 0.9 collective-permute-done.18
  248.7 4.4 %collective-permute-start.19 = (f32[1,32,128]{2,1,0:T(8,128)S(1)}, f32[1,32,128]{2,1,0:T(8,128)S(1)}, u32[]{:S(2)}, u32[]{:S(2)}) collective-permute-start(f32[1,32,128]{2,1,0:T(8,128)S(1)} %constant_dynamic-slice_fusion), channel_id=1, source_target_pairs={{0,32},{4,36},{8,40},{12,44},{16,48},{20,52},{24,56},{28,60},{32,0... | collective-permute-start | bytes 49160 | tf_op jit(solution)/shard_map/ppermute | solution.py:23
  253.8 2.7 collective-permute-done.19
  257.2 1.3 exponential_reduce_fusion.1
  259.1 2.5 multiply_reduce_fusion.2
  261.6 1.2 collective-permute-done.20
  264.1 1.7 collective-permute-start.21
  265.7 2.2 collective-permute-done.21
  268.6 2.5 collective-permute-start.22
  271.1 1.1 collective-permute-done.22
  272.9 3.9 %collective-permute-start.23 = (f32[]{:T(128)}, f32[]{:T(128)}, u32[]{:S(2)}, u32[]{:S(2)}) collective-permute-start(f32[]{:T(128)} %add.182), channel_id=1, source_target_pairs={{0,16},{4,20},{8,24},{12,28},{16,0},{20,4},{24,8},{28,12},{32,48},... | collective-permute-start | bytes 20 | tf_op jit(solution)/shard_map/ppermute | solution.py:23
  278.1 4.1 %collective-permute-start.24 = (f32[]{:T(128)}, f32[]{:T(128)}, u32[]{:S(2)}, u32[]{:S(2)}) collective-permute-start(f32[]{:T(128)} %add.183), channel_id=1, source_target_pairs={{0,128},{4,132},{8,136},{12,140},{16,144},{20,148},{24,152},{28,15... | collective-permute-start | bytes 20 | tf_op jit(solution)/shard_map/ppermute | solution.py:23
  282.3 1.0 collective-permute-done.24
  283.9 5.6 %collective-permute-start.25 = (f32[]{:T(128)}, f32[]{:T(128)}, u32[]{:S(2)}, u32[]{:S(2)}) collective-permute-start(f32[]{:T(128)} %add.184), channel_id=1, source_target_pairs={{0,32},{4,36},{8,40},{12,44},{16,48},{20,52},{24,56},{28,60},{32,0... | collective-permute-start | bytes 20 | tf_op jit(solution)/shard_map/ppermute | solution.py:23
  289.6 1.9 collective-permute-done.25
  292.1 1.4 collective-permute-start.26
  293.5 2.2 collective-permute-done.26
  296.4 3.0 collective-permute-start.27
  299.4 2.1 collective-permute-done.27
  (86 shorter events, 10.4 us)
Async XLA Ops:
  7.2 2.3 copy-start
  7.2 191.3 %all-gather.2.cloned.1.call-start = ((), (), s32[]{:S(2)}) async-start(), calls=%async_computation | async-start | bytes 8519680 | tf_op jit(solution)/shard_map/all_gather | solution.py:142
  9.4 2.2 copy-start.2
  9.5 2.2 copy-start.8
  9.5 2.2 copy-start.9
  12.5 23.6 %collective-permute-start = (bf16[2,256,512]{2,1,0:T(8,128)(2,1)S(1)}, bf16[2,256,512]{2,1,0:T(8,128)(2,1)}, u32[]{:S(2)}, u32[]{:S(2)}) collective-permute-start(bf16[2,256,512]{2,1,0:T(8,128)(2,1)S(1)} %pad_maximum_fusion), channel_id=1, source_target_pairs={{0,16},{4,20},{8,24},{12,28},{16,32},{20,36},{24,40},{28,44},{32,4... | collective-permute-start | bytes 1572872 | tf_op jit(solution)/shard_map/ppermute | solution.py:18
  18.5 43.7 %collective-permute-start.1 = (bf16[2,256,512]{2,1,0:T(8,128)(2,1)S(1)}, bf16[2,256,512]{2,1,0:T(8,128)(2,1)}, u32[]{:S(2)}, u32[]{:S(2)}) collective-permute-start(bf16[2,256,512]{2,1,0:T(8,128)(2,1)S(1)} %pad_maximum_fusion), channel_id=1, source_target_pairs={{0,12},{4,16},{8,20},{12,24},{16,28},{20,32},{24,36},{28,40},{32,4... | collective-permute-start | bytes 1572872 | tf_op jit(solution)/shard_map/ppermute | solution.py:18
  22.3 56.5 %collective-permute-start.2 = (bf16[2,256,512]{2,1,0:T(8,128)(2,1)S(1)}, bf16[2,256,512]{2,1,0:T(8,128)(2,1)}, u32[]{:S(2)}, u32[]{:S(2)}) collective-permute-start(bf16[2,256,512]{2,1,0:T(8,128)(2,1)S(1)} %pad_maximum_fusion), channel_id=1, source_target_pairs={{0,8},{4,12},{8,16},{12,20},{16,24},{20,28},{24,32},{28,36},{32,40... | collective-permute-start | bytes 1572872 | tf_op jit(solution)/shard_map/ppermute | solution.py:18
  27.3 53.8 %collective-permute-start.3 = (bf16[2,256,512]{2,1,0:T(8,128)(2,1)S(1)}, bf16[2,256,512]{2,1,0:T(8,128)(2,1)S(1)}, u32[]{:S(2)}, u32[]{:S(2)}) collective-permute-start(bf16[2,256,512]{2,1,0:T(8,128)(2,1)S(1)} %pad_maximum_fusion), channel_id=1, source_target_pairs={{0,4},{4,8},{8,12},{12,16},{16,20},{20,24},{24,28},{28,32},{32,36}... | collective-permute-start | bytes 1572872 | tf_op jit(solution)/shard_map/ppermute | solution.py:18
  29.6 53.2 %collective-permute-start.4 = (bf16[2,256,512]{2,1,0:T(8,128)(2,1)S(1)}, bf16[2,256,512]{2,1,0:T(8,128)(2,1)S(1)}, u32[]{:S(2)}, u32[]{:S(2)}) collective-permute-start(bf16[2,256,512]{2,1,0:T(8,128)(2,1)S(1)} %pad_maximum_fusion), channel_id=1, source_target_pairs={{4,0},{8,4},{12,8},{16,12},{20,16},{24,20},{28,24},{32,28},{36,32}... | collective-permute-start | bytes 1572872 | tf_op jit(solution)/shard_map/ppermute | solution.py:18
  32.6 3.1 copy-start.5
  36.1 47.9 %collective-permute-start.5 = (bf16[2,256,512]{2,1,0:T(8,128)(2,1)S(1)}, bf16[2,256,512]{2,1,0:T(8,128)(2,1)S(1)}, u32[]{:S(2)}, u32[]{:S(2)}) collective-permute-start(bf16[2,256,512]{2,1,0:T(8,128)(2,1)S(1)} %pad_maximum_fusion), channel_id=1, source_target_pairs={{8,0},{12,4},{16,8},{20,12},{24,16},{28,20},{32,24},{36,28},{40,32... | collective-permute-start | bytes 1572872 | tf_op jit(solution)/shard_map/ppermute | solution.py:18
  62.2 24.5 %collective-permute-start.6 = (bf16[2,256,512]{2,1,0:T(8,128)(2,1)S(1)}, bf16[2,256,512]{2,1,0:T(8,128)(2,1)S(1)}, u32[]{:S(2)}, u32[]{:S(2)}) collective-permute-start(bf16[2,256,512]{2,1,0:T(8,128)(2,1)S(1)} %pad_maximum_fusion), channel_id=1, source_target_pairs={{12,0},{16,4},{20,8},{24,12},{28,16},{32,20},{36,24},{40,28},{44,3... | collective-permute-start | bytes 1572872 | tf_op jit(solution)/shard_map/ppermute | solution.py:18
  78.8 48.7 %collective-permute-start.7 = (bf16[2,256,512]{2,1,0:T(8,128)(2,1)S(1)}, bf16[2,256,512]{2,1,0:T(8,128)(2,1)S(1)}, u32[]{:S(2)}, u32[]{:S(2)}) collective-permute-start(bf16[2,256,512]{2,1,0:T(8,128)(2,1)S(1)} %pad_maximum_fusion), channel_id=1, source_target_pairs={{16,0},{20,4},{24,8},{28,12},{32,16},{36,20},{40,24},{44,28},{48,3... | collective-permute-start | bytes 1572872 | tf_op jit(solution)/shard_map/ppermute | solution.py:18
  81.2 112.0 %collective-permute-start.11 = (bf16[512,2048]{1,0:T(8,128)(2,1)}, bf16[512,2048]{1,0:T(8,128)(2,1)}, u32[]{:S(2)}, u32[]{:S(2)}) collective-permute-start(bf16[512,2048]{1,0:T(8,128)(2,1)} %param.15), channel_id=1, source_target_pairs={{0,1},{1,2},{2,3},{3,0},{4,5},{5,6},{6,7},{7,4},{8,9},{9,10},{10,1... | collective-permute-start | bytes 6291464 | tf_op jit(solution)/shard_map/ppermute | solution.py:28
  82.8 110.4 %collective-permute-start.12 = (bf16[512,2048]{1,0:T(8,128)(2,1)}, bf16[512,2048]{1,0:T(8,128)(2,1)}, u32[]{:S(2)}, u32[]{:S(2)}) collective-permute-start(bf16[512,2048]{1,0:T(8,128)(2,1)} %param.15), channel_id=1, source_target_pairs={{0,2},{1,3},{2,0},{3,1},{4,6},{5,7},{6,4},{7,5},{8,10},{9,11},{10,... | collective-permute-start | bytes 6291464 | tf_op jit(solution)/shard_map/ppermute | solution.py:28
  84.1 109.1 %collective-permute-start.13 = (bf16[512,2048]{1,0:T(8,128)(2,1)}, bf16[512,2048]{1,0:T(8,128)(2,1)}, u32[]{:S(2)}, u32[]{:S(2)}) collective-permute-start(bf16[512,2048]{1,0:T(8,128)(2,1)} %param.15), channel_id=1, source_target_pairs={{0,3},{1,0},{2,1},{3,2},{4,7},{5,4},{6,5},{7,6},{8,11},{9,8},{10,9... | collective-permute-start | bytes 6291464 | tf_op jit(solution)/shard_map/ppermute | solution.py:28
  152.1 31.2 %collective-permute-start.10 = (bf16[256,512]{0,1:T(8,128)(2,1)S(1)}, bf16[256,512]{0,1:T(8,128)(2,1)S(1)}, u32[]{:S(2)}, u32[]{:S(2)}) collective-permute-start(bf16[256,512]{0,1:T(8,128)(2,1)S(1)} %bitcast.68), channel_id=1, source_target_pairs={{0,3},{1,0},{2,1},{3,2},{4,7},{5,4},{6,5},{7,6},{8,11},{9,8},{10,9... | collective-permute-start | bytes 786440 | tf_op jit(solution)/shard_map/ppermute | solution.py:28
  153.0 31.8 %collective-permute-start.8 = (bf16[256,512]{0,1:T(8,128)(2,1)S(1)}, bf16[256,512]{0,1:T(8,128)(2,1)S(1)}, u32[]{:S(2)}, u32[]{:S(2)}) collective-permute-start(bf16[256,512]{0,1:T(8,128)(2,1)S(1)} %bitcast.69), channel_id=1, source_target_pairs={{0,1},{1,2},{2,3},{3,0},{4,5},{5,6},{6,7},{7,4},{8,9},{9,10},{10,1... | collective-permute-start | bytes 786440 | tf_op jit(solution)/shard_map/ppermute | solution.py:28
  183.4 9.8 %collective-permute-start.9 = (bf16[256,512]{0,1:T(8,128)(2,1)S(1)}, bf16[256,512]{0,1:T(8,128)(2,1)S(1)}, u32[]{:S(2)}, u32[]{:S(2)}) collective-permute-start(bf16[256,512]{0,1:T(8,128)(2,1)S(1)} %bitcast.70), channel_id=1, source_target_pairs={{0,2},{1,3},{2,0},{3,1},{4,6},{5,7},{6,4},{7,5},{8,10},{9,11},{10,... | collective-permute-start | bytes 786440 | tf_op jit(solution)/shard_map/ppermute | solution.py:28
  184.8 13.4 %copy-start.4 = (f32[2048]{0:T(1024)S(1)}, f32[2048]{0:T(1024)}, u32[]{:S(2)}) copy-start(f32[2048]{0:T(1024)} %param.17) | copy-start | bytes 24580
  198.4 6.2 %copy-start.3 = (bf16[256,2048]{1,0:T(8,128)(2,1)}, bf16[256,2048]{1,0:T(8,128)(2,1)S(1)}, u32[]{:S(2)}) copy-start(bf16[256,2048]{1,0:T(8,128)(2,1)S(1)} %multiply_convert_fusion) | copy-start | bytes 3145732
  210.5 29.8 %copy-start.7 = (f32[1,128]{1,0:T(1,128)S(1)}, f32[1,128]{1,0:T(1,128)}, u32[]{:S(2)}) copy-start(f32[1,128]{1,0:T(1,128)} %param.21) | copy-start | bytes 1540
  210.5 2.3 collective-permute-start.14
  210.5 91.7 %copy-start.1 = (bf16[2048,512]{1,0:T(8,128)(2,1)S(1)}, bf16[2048,512]{1,0:T(8,128)(2,1)}, u32[]{:S(2)}) copy-start(bf16[2048,512]{1,0:T(8,128)(2,1)} %param.13) | copy-start | bytes 6291460
  215.7 13.1 %collective-permute-start.15 = (f32[16,32,128]{2,1,0:T(8,128)S(1)}, f32[16,32,128]{2,1,0:T(8,128)S(1)}, u32[]{:S(2)}, u32[]{:S(2)}) collective-permute-start(f32[16,32,128]{2,1,0:T(8,128)S(1)} %constant_dynamic-slice_fusion.4), channel_id=1, source_target_pairs={{0,8},{4,12},{8,0},{12,4},{16,24},{20,28},{24,16},{28,20},{32,40},... | collective-permute-start | bytes 786440 | tf_op jit(solution)/shard_map/ppermute | solution.py:23
  229.8 5.1 %collective-permute-start.16 = (f32[8,32,128]{2,1,0:T(8,128)S(1)}, f32[8,32,128]{2,1,0:T(8,128)S(1)}, u32[]{:S(2)}, u32[]{:S(2)}) collective-permute-start(f32[8,32,128]{2,1,0:T(8,128)S(1)} %constant_dynamic-slice_fusion.3), channel_id=1, source_target_pairs={{0,64},{4,68},{8,72},{12,76},{16,80},{20,84},{24,88},{28,92},{32,9... | collective-permute-start | bytes 393224 | tf_op jit(solution)/shard_map/ppermute | solution.py:23
  234.9 8.3 %collective-permute-start.17 = (f32[4,32,128]{2,1,0:T(8,128)S(1)}, f32[4,32,128]{2,1,0:T(8,128)S(1)}, u32[]{:S(2)}, u32[]{:S(2)}) collective-permute-start(f32[4,32,128]{2,1,0:T(8,128)S(1)} %constant_dynamic-slice_fusion.2), channel_id=1, source_target_pairs={{0,16},{4,20},{8,24},{12,28},{16,0},{20,4},{24,8},{28,12},{32,48},... | collective-permute-start | bytes 196616 | tf_op jit(solution)/shard_map/ppermute | solution.py:23
  243.2 5.5 %collective-permute-start.18 = (f32[2,32,128]{2,1,0:T(8,128)S(1)}, f32[2,32,128]{2,1,0:T(8,128)S(1)}, u32[]{:S(2)}, u32[]{:S(2)}) collective-permute-start(f32[2,32,128]{2,1,0:T(8,128)S(1)} %constant_dynamic-slice_fusion.1), channel_id=1, source_target_pairs={{0,128},{4,132},{8,136},{12,140},{16,144},{20,148},{24,152},{28,15... | collective-permute-start | bytes 98312 | tf_op jit(solution)/shard_map/ppermute | solution.py:23
  248.7 7.8 %collective-permute-start.19 = (f32[1,32,128]{2,1,0:T(8,128)S(1)}, f32[1,32,128]{2,1,0:T(8,128)S(1)}, u32[]{:S(2)}, u32[]{:S(2)}) collective-permute-start(f32[1,32,128]{2,1,0:T(8,128)S(1)} %constant_dynamic-slice_fusion), channel_id=1, source_target_pairs={{0,32},{4,36},{8,40},{12,44},{16,48},{20,52},{24,56},{28,60},{32,0... | collective-permute-start | bytes 49160 | tf_op jit(solution)/shard_map/ppermute | solution.py:23
  257.2 45.1 %copy-start.6 = (f32[128]{0:T(128)}, f32[128]{0:T(128)S(1)}, u32[]{:S(2)}) copy-start(f32[128]{0:T(128)S(1)} %get-tuple-element.7) | copy-start | bytes 1540
  261.6 1.2 collective-permute-start.20
  264.1 3.9 %collective-permute-start.21 = (f32[]{:T(128)}, f32[]{:T(128)}, u32[]{:S(2)}, u32[]{:S(2)}) collective-permute-start(f32[]{:T(128)} %add.180), channel_id=1, source_target_pairs={{0,8},{4,12},{8,0},{12,4},{16,24},{20,28},{24,16},{28,20},{32,40},... | collective-permute-start | bytes 20 | tf_op jit(solution)/shard_map/ppermute | solution.py:23
  268.6 3.6 %collective-permute-start.22 = (f32[]{:T(128)}, f32[]{:T(128)}, u32[]{:S(2)}, u32[]{:S(2)}) collective-permute-start(f32[]{:T(128)} %add.181), channel_id=1, source_target_pairs={{0,64},{4,68},{8,72},{12,76},{16,80},{20,84},{24,88},{28,92},{32,9... | collective-permute-start | bytes 20 | tf_op jit(solution)/shard_map/ppermute | solution.py:23
  272.9 4.5 %collective-permute-start.23 = (f32[]{:T(128)}, f32[]{:T(128)}, u32[]{:S(2)}, u32[]{:S(2)}) collective-permute-start(f32[]{:T(128)} %add.182), channel_id=1, source_target_pairs={{0,16},{4,20},{8,24},{12,28},{16,0},{20,4},{24,8},{28,12},{32,48},... | collective-permute-start | bytes 20 | tf_op jit(solution)/shard_map/ppermute | solution.py:23
  278.1 5.1 %collective-permute-start.24 = (f32[]{:T(128)}, f32[]{:T(128)}, u32[]{:S(2)}, u32[]{:S(2)}) collective-permute-start(f32[]{:T(128)} %add.183), channel_id=1, source_target_pairs={{0,128},{4,132},{8,136},{12,140},{16,144},{20,148},{24,152},{28,15... | collective-permute-start | bytes 20 | tf_op jit(solution)/shard_map/ppermute | solution.py:23
  283.9 7.5 %collective-permute-start.25 = (f32[]{:T(128)}, f32[]{:T(128)}, u32[]{:S(2)}, u32[]{:S(2)}) collective-permute-start(f32[]{:T(128)} %add.184), channel_id=1, source_target_pairs={{0,32},{4,36},{8,40},{12,44},{16,48},{20,52},{24,56},{28,60},{32,0... | collective-permute-start | bytes 20 | tf_op jit(solution)/shard_map/ppermute | solution.py:23
  292.1 3.6 %collective-permute-start.26 = (f32[]{:T(128)}, f32[]{:T(128)}, u32[]{:S(2)}, u32[]{:S(2)}) collective-permute-start(f32[]{:T(128)} %add.185), channel_id=1, source_target_pairs={{0,1},{1,0},{2,3},{3,2},{4,5},{5,4},{6,7},{7,6},{8,9},{9,8},{10,11... | collective-permute-start | bytes 20 | tf_op jit(solution)/shard_map/ppermute | solution.py:23
  296.4 5.1 %collective-permute-start.27 = (f32[]{:T(128)}, f32[]{:T(128)}, u32[]{:S(2)}, u32[]{:S(2)}) collective-permute-start(f32[]{:T(128)} %add.186), channel_id=1, source_target_pairs={{0,2},{1,3},{2,0},{3,1},{4,6},{5,7},{6,4},{7,5},{8,10},{9,11},{10,... | collective-permute-start | bytes 20 | tf_op jit(solution)/shard_map/ppermute | solution.py:23
Sparse Core Ops, SparseCore 0:
  10.8 115.7 all-gather.1

commit v2 on v1

--- a/solution.py
+++ b/solution.py
@@ -3,6 +3,7 @@
 from jax import lax
 from jax.sharding import PartitionSpec as P
 
+
 HD = 128
 WIN = 2048
 LQ = 32
@@ -12,9 +13,13 @@
 SOFTMAX_TEMP = 0.1
 
 
-def shifted_2(x, axis, by):
-    count = lax.axis_size(axis)
-    pairs = [(i, i + by) for i in range(count) if 0 <= i + by < count]
+def sided_fetch(x, axis, distance):
+    count = lax.axis_size(axis)
+    pairs = []
+    for target in range(count):
+        source = target - distance if target % 2 == 0 else target + distance
+        if 0 <= source < count:
+            pairs.append((source, target))
     return lax.ppermute(x, axis, pairs)
 
 
@@ -98,36 +103,49 @@
     total_tokens = shard_rows * seq_count
     residual = tokens.astype(jnp.float32)
     normed = rms_scale(residual, gain_attn).astype(jnp.bfloat16)
+    pb_count = lax.axis_size("pb")
+    w_out_parts = [w_out] + [ring_shift(w_out, "pb", k) for k in range(1, pb_count)]
     q_local = jnp.dot(normed, w_query, preferred_element_type=jnp.float32).astype(jnp.bfloat16)
     k_local = jnp.dot(normed, w_key, preferred_element_type=jnp.float32).astype(jnp.bfloat16)
     v_local = jnp.dot(normed, w_value, preferred_element_type=jnp.float32).astype(jnp.bfloat16)
-    key_value = jnp.stack([k_local, v_local])
-    earlier = [shifted_2(key_value, "seq", distance) for distance in range(reach_count, 0, -1)]
-    later = [shifted_2(key_value, "seq", -distance) for distance in range(1, reach_count + 1)]
-    window = jnp.concatenate(earlier + [key_value] + later, axis=1)
-    span_rows = window.shape[1]
+    core = seq_place % 2
+    toward = 2 * core - 1
+    k_heads_local = k_local.reshape(shard_rows, heads_here, HD).transpose(1, 0, 2)
+    v_heads_local = v_local.reshape(shard_rows, heads_here, HD).transpose(1, 0, 2)
+    key_value = jnp.stack([k_heads_local, v_heads_local])
+    fetched = [sided_fetch(key_value, "seq", distance) for distance in range(1, reach_count + 1)]
+    handed = lax.ppermute(
+        jnp.stack([key_value] + fetched[: reach_count - 1]),
+        "seq",
+        [(i, i ^ 1) for i in range(seq_count)],
+    )
+    blocks = [key_value] + fetched + [handed[j] for j in range(reach_count)]
+    window = jnp.concatenate(blocks, axis=2)
+    span_rows = window.shape[2]
+    block_shift = jnp.asarray(
+        [0] + list(range(1, reach_count + 1)) + [-d for d in range(1, reach_count + 1)], jnp.int32
+    )
+    block_start = (seq_place + toward * block_shift) * shard_rows
     q_pos = my_start + jnp.arange(shard_rows, dtype=jnp.int32)
-    k_pos = my_start - reach_count * shard_rows + jnp.arange(span_rows, dtype=jnp.int32)
+    k_pos = (block_start[:, None] + jnp.arange(shard_rows, dtype=jnp.int32)[None, :]).reshape(span_rows)
     in_window = (
         (jnp.abs(q_pos[:, None] - k_pos[None, :]) <= half_win)
         & (k_pos >= 0)[None, :]
         & (k_pos < total_tokens)[None, :]
     )
-    q_heads = q_local.reshape(shard_rows, heads_here, HD)
-    k_heads = window[0].reshape(span_rows, heads_here, HD)
-    v_heads = window[1].reshape(span_rows, heads_here, HD)
+    q_heads = q_local.reshape(shard_rows, heads_here, HD).transpose(1, 0, 2)
+    k_heads = window[0]
+    v_heads = window[1]
     logits = jnp.einsum(
-        "qhd,khd->hqk", q_heads, k_heads, preferred_element_type=jnp.float32
+        "hqd,hkd->hqk", q_heads, k_heads, preferred_element_type=jnp.float32
     ) * HD ** (-0.5)
     logits = jnp.where(in_window[None], logits, -jnp.inf)
     row_max = jnp.max(logits, axis=-1, keepdims=True)
     exp_terms = jnp.exp(logits - row_max)
     weights = (exp_terms / jnp.sum(exp_terms, axis=-1, keepdims=True)).astype(jnp.bfloat16)
-    mixed = jnp.einsum("hqk,khd->qhd", weights, v_heads, preferred_element_type=jnp.float32)
+    mixed = jnp.einsum("hqk,hkd->qhd", weights, v_heads, preferred_element_type=jnp.float32)
     mixed = mixed.reshape(shard_rows, head_width).astype(jnp.bfloat16)
-    pb_count = lax.axis_size("pb")
     mixed_parts = [mixed] + [ring_shift(mixed, "pb", k) for k in range(1, pb_count)]
-    w_out_parts = [w_out] + [ring_shift(w_out, "pb", k) for k in range(1, pb_count)]
     attn_sum = jnp.dot(
         jnp.concatenate(mixed_parts, axis=1),
         jnp.concatenate(w_out_parts, axis=0),
@@ -187,6 +205,7 @@
         P(),
         P(("seq", "pb"), None),
     )
+
     return jax.shard_map(
         per_device,
         mesh=mesh,

time: 311 us -> 251 us (0.81)
  waiting for transfers between devices: 147 us -> 44.1 us
  starting transfers between devices: 73.5 us -> 121 us
  local copies, waits for them, and re-layouts: 17.3 us -> 13.4 us
  matrix products: 32 us -> 28.3 us
    ppermute x8 -> x5, waiting for transfers between devices: 78.7 us -> 7.55 us  [the longest x4 7.54 us: sided_fetch(): return lax.ppermute(x, axis, pairs)]
    ppermute x6, starting transfers between devices: 8.85 us -> 48.8 us  [ring_shift(): return lax.ppermute(x, axis, [(i, (i + by) % count) for i in range(count)])]
    ppermute x6, waiting for transfers between devices: 37.3 us -> 4.58 us  [ring_shift(): return lax.ppermute(x, axis, [(i, (i + by) % count) for i in range(count)])]
    another operation x2 -> x1, local copies, waits for them, and re-layouts: 7.84 us -> 0.09 us  [per_device(): key_value = jnp.stack([k_heads_local, v_heads_local])]
    ppermute x8 -> x5, starting transfers between devices: 22.2 us -> 28.9 us  [the longest x1 15.3 us: per_device(): lax.ppermute(jnp.stack([key_value] + fetched[:reach_count - 1]), 'seq', [...]
    unnamed x27 -> x37, local copies, waits for them, and re-layouts: 3.51 us -> 8.26 us
    sub x1, matrix products: 8.86 us -> 4.89 us  [per_device(): exp_terms = jnp.exp(logits - row_max)]
  transfers between devices with their start and end apart: 29 -> 26, of which waited for: 19 -> 17; matrix products, arithmetic and copies ran while one was open for 14% -> 16% of each run, Pallas kernels for 0% -> 0%
where the time goes in v2:
time: 251 us; the launch traced here: 248 us
  starting transfers between devices  121 us (48%)
  waiting for transfers between devices  44.1 us (18%)
  matrix products  28.3 us (11%)
  between operations  22.9 us (9%)
  other arithmetic  19 us (8%)
  local copies, waits for them, and re-layouts  13.4 us (5%)
    ppermute x6, starting transfers between devices, ring_shift(): return lax.ppermute(x, axis, [(i, (i + by) % count) for i in range(count)])  48.8 us
    ppermute x14, starting transfers between devices, xor_swap(): return lax.ppermute(x, axis, [(i, i ^ bit) for i in range(count)])  42.9 us
    ppermute x14, waiting for transfers between devices, xor_swap(): return lax.ppermute(x, axis, [(i, i ^ bit) for i in range(count)])  31.3 us
    ppermute x1, starting transfers between devices, per_device(): lax.ppermute(jnp.stack([key_value] + fetched[:reach_count - 1]), 'seq', [...  15.3 us
    ppermute x4, starting transfers between devices, sided_fetch(): return lax.ppermute(x, axis, pairs)  13.6 us
    unnamed x37, local copies, waits for them, and re-layouts  8.26 us
    ppermute x4, waiting for transfers between devices, sided_fetch(): return lax.ppermute(x, axis, pairs)  7.54 us
    dot_general x1, matrix products, per_device(): jnp.einsum('hqk,hkd->qhd', weights, v_heads, preferred_element_type=jnp.f...  6.8 us
  transfers between devices with their start and end apart: 26, of which 17 were waited for; matrix products, arithmetic and copies ran while one was open for 16% of the time, Pallas kernels for 0%

profile of v2, /device:TPU:2, one launch (start us, length us, event | category | flops | bytes accessed | tf_op | source)
XLA Modules:
  0.0 248.2 jit_solution(945824369343110425)
XLA Ops:
  7.2 0.7 all-gather.2.cloned.1.call-update
  7.9 1.5 fusion.19
  9.5 2.1 fusion.23
  11.7 0.8 fusion.24
  12.6 1.3 fusion.48
  13.9 0.7 collective-permute-start
  14.6 5.1 %collective-permute-start.1 = (bf16[2,4,256,128]{3,2,1,0:T(8,128)(2,1)}, bf16[2,4,256,128]{3,2,1,0:T(8,128)(2,1)S(1)}, u32[]{:S(2)}, u32[]{:S(2)}) collective-permute-start(bf16[2,4,256,128]{3,2,1,0:T(8,128)(2,1)} %get-tuple-element.10), channel_id=1, source_target_pairs={{12,4},{0,8},{20,12},{8,16},{28,20},{16,24},{36,28},{24,32},{44,36... | collective-permute-start | bytes 1572872 | tf_op jit(solution)/shard_map/ppermute | solution.py:23
  19.7 0.7 collective-permute-start.2
  20.4 7.2 %collective-permute-start.3 = (bf16[2,4,256,128]{3,2,1,0:T(8,128)(2,1)}, bf16[2,4,256,128]{3,2,1,0:T(8,128)(2,1)}, u32[]{:S(2)}, u32[]{:S(2)}) collective-permute-start(bf16[2,4,256,128]{3,2,1,0:T(8,128)(2,1)} %get-tuple-element.10), channel_id=1, source_target_pairs={{20,4},{28,12},{0,16},{36,20},{8,24},{44,28},{16,32},{52,36},{24,4... | collective-permute-start | bytes 1572872 | tf_op jit(solution)/shard_map/ppermute | solution.py:23
  28.6 1.5 collective-permute-start.8
  30.1 7.5 %collective-permute-done.1 = bf16[2,4,256,128]{3,2,1,0:T(8,128)(2,1)S(1)} collective-permute-done((bf16[2,4,256,128]{3,2,1,0:T(8,128)(2,1)}, bf16[2,4,256,128]{3,2,1,0:T(8,128)(2,1)S(1)}, u32[]{:S(2)}, u32[]{:S(2)}) %collective-permute-start.1) | collective-permute-done | bytes 524320 | tf_op jit(solution)/shard_map/ppermute | solution.py:23
  37.7 2.1 collective-permute-start.9
  39.8 0.8 copy-done.2
  40.6 1.6 pad_maximum_fusion
  42.2 15.3 %collective-permute-start.4 = (bf16[4,2,4,256,128]{4,3,2,1,0:T(8,128)(2,1)}, bf16[4,2,4,256,128]{4,3,2,1,0:T(8,128)(2,1)S(1)}, u32[]{:S(2)}, u32[]{:S(2)}) collective-permute-start(bf16[4,2,4,256,128]{4,3,2,1,0:T(8,128)(2,1)} %pad_maximum_fusion), channel_id=1, source_target_pairs={{0,4},{4,0},{8,12},{12,8},{16,20},{20,16},{24,28},{28,24},{32,36},... | collective-permute-start | bytes 6291464 | tf_op jit(solution)/shard_map/ppermute | solution.py:117
  57.4 2.7 %fusion.25 = bf16[32,4,8,128]{3,2,1,0:T(8,128)(2,1)S(1)} fusion(bf16[2048,512]{1,0:T(8,128)(2,1)} %param.13, bf16[256,2048]{1,0:T(8,128)(2,1)} %param.12, f32[2048]{0:T(1024)S(1)} %copy-done.14, f32[256]{0:T(256)S(1)} %add_rsqrt_fusion.1), kind=kOutput, calls=%fused_computation.48 | convolution fusion | flops 539099136 | bytes 3417088 | tf_op jit(solution)/shard_map/dot_general | solution.py:108
  60.1 1.7 fusion.18
  62.0 0.9 constant_dynamic-update-slice_fusion.3
  62.9 0.9 constant_dynamic-update-slice_fusion.2
  63.8 0.9 constant_dynamic-update-slice_fusion.1
  64.7 2.0 constant_dynamic-update-slice_fusion
  66.6 0.9 fusion.36
  67.5 0.9 fusion.35
  68.4 0.9 fusion.34
  69.3 0.9 fusion.33
  70.2 4.9 %fusion.52 = f32[4,256]{1,0:T(4,128)S(1)} fusion(pred[256,2304]{1,0:T(8,128)(4,1)S(1)} %copy-done.7, bf16[2,4,2304,128]{3,2,1,0:T(8,128)(2,1)} %fusion.33, bf16[32,4,8,128]{3,2,1,0:T(8,128)(2,1)S(1)} %fusion.25), kind=kOutput, calls=%fused_computation.126 | convolution fusion | flops 613419264 | bytes 3215360 | tf_op jit(solution)/shard_map/sub | solution.py:144
  75.1 6.8 %fusion.22 = bf16[4,128,256]{2,1,0:T(8,128)(2,1)S(1)} fusion(f32[4,256]{1,0:T(4,128)S(1)} %fusion.52, bf16[2,4,2304,128]{3,2,1,0:T(8,128)(2,1)} %fusion.33, pred[256,2304]{1,0:T(8,128)(4,1)S(1)} %copy-done.7, bf16[32,4,8,128]{3,2,1,0:T(8,128)(2,1)S(1)} %fusion.25), kind=kOutput, calls=%fused_computation.42 | convolution fusion | flops 1219890432 | bytes 5836800 | tf_op jit(solution)/shard_map/hqk,hkd->qhd/dot_general | solution.py:146
  81.9 2.0 collective-permute-start.5
  83.9 1.1 collective-permute-start.6
  85.0 41.5 %collective-permute-start.7 = (bf16[256,512]{0,1:T(8,128)(2,1)S(1)}, bf16[256,512]{0,1:T(8,128)(2,1)S(1)}, u32[]{:S(2)}, u32[]{:S(2)}) collective-permute-start(bf16[256,512]{0,1:T(8,128)(2,1)S(1)} %bitcast.139), channel_id=1, source_target_pairs={{0,3},{1,0},{2,1},{3,2},{4,7},{5,4},{6,5},{7,6},{8,11},{9,8},{10,9... | collective-permute-start | bytes 786440 | tf_op jit(solution)/shard_map/ppermute | solution.py:33
  126.6 2.1 collective-permute-done.5
  128.7 2.5 %collective-permute-done.7 = bf16[256,512]{0,1:T(8,128)(2,1)S(1)} collective-permute-done((bf16[256,512]{0,1:T(8,128)(2,1)S(1)}, bf16[256,512]{0,1:T(8,128)(2,1)S(1)}, u32[]{:S(2)}, u32[]{:S(2)}) %collective-permute-start.7) | collective-permute-done | bytes 262176 | tf_op jit(solution)/shard_map/ppermute | solution.py:33
  131.2 4.9 %multiply_reduce_fusion = (f32[256]{0:T(256)S(1)}, f32[256,2048]{1,0:T(8,128)S(1)}) fusion(bf16[512,2048]{1,0:T(8,128)(2,1)} %collective-permute-done.10, bf16[512,2048]{1,0:T(8,128)(2,1)} %collective-permute-done.9, bf16[512,2048]{1,0:T(8,128)(2,1)} %collective-permute-done.8, bf16[512,2048]{1,0:T(8,128)(2,1)} %param.16, ...), kind=kOutput, calls=%fused_computation.41 | convolution fusion | flops 2187329280 | bytes 12583936 | tf_op jit(solution)/shard_map/dot_general | solution.py:149
  136.4 6.1 %convolution_bitcast_fusion = f32[2048,256]{0,1:T(8,128)S(1)} fusion(bf16[256,2048]{1,0:T(8,128)(2,1)S(1)} %multiply_convert_fusion, bf16[2048,2048]{1,0:T(8,128)(2,1)} %bitcast.136), kind=kOutput, calls=%fused_computation.29 | convolution fusion | flops 2147483648 | bytes 11534336 | tf_op jit(solution)/shard_map/td,rd->tr/dot_general | solution.py:163
  146.1 1.0 gather_fusion
  147.7 0.8 constant_dynamic-slice_fusion.5
  148.5 2.2 collective-permute-done.11
  150.7 1.9 dynamic-slice_maximum_fusion
  152.7 1.0 constant_dynamic-slice_fusion.4
  153.6 3.2 %collective-permute-start.12 = (f32[16,32,128]{2,1,0:T(8,128)S(1)}, f32[16,32,128]{2,1,0:T(8,128)S(1)}, u32[]{:S(2)}, u32[]{:S(2)}) collective-permute-start(f32[16,32,128]{2,1,0:T(8,128)S(1)} %constant_dynamic-slice_fusion.4), channel_id=1, source_target_pairs={{0,8},{4,12},{8,0},{12,4},{16,24},{20,28},{24,16},{28,20},{32,40},... | collective-permute-start | bytes 786440 | tf_op jit(solution)/shard_map/ppermute | solution.py:28
  156.8 6.6 %collective-permute-done.12 = f32[16,32,128]{2,1,0:T(8,128)S(1)} collective-permute-done((f32[16,32,128]{2,1,0:T(8,128)S(1)}, f32[16,32,128]{2,1,0:T(8,128)S(1)}, u32[]{:S(2)}, u32[]{:S(2)}) %collective-permute-start.12) | collective-permute-done | bytes 262176 | tf_op jit(solution)/shard_map/ppermute | solution.py:28
  163.5 1.0 dynamic-slice_maximum_fusion.1
  164.5 4.4 %collective-permute-start.13 = (f32[8,32,128]{2,1,0:T(8,128)S(1)}, f32[8,32,128]{2,1,0:T(8,128)S(1)}, u32[]{:S(2)}, u32[]{:S(2)}) collective-permute-start(f32[8,32,128]{2,1,0:T(8,128)S(1)} %constant_dynamic-slice_fusion.3), channel_id=1, source_target_pairs={{0,64},{4,68},{8,72},{12,76},{16,80},{20,84},{24,88},{28,92},{32,9... | collective-permute-start | bytes 393224 | tf_op jit(solution)/shard_map/ppermute | solution.py:28
  168.9 2.9 %collective-permute-done.13 = f32[8,32,128]{2,1,0:T(8,128)S(1)} collective-permute-done((f32[8,32,128]{2,1,0:T(8,128)S(1)}, f32[8,32,128]{2,1,0:T(8,128)S(1)}, u32[]{:S(2)}, u32[]{:S(2)}) %collective-permute-start.13) | collective-permute-done | bytes 131104 | tf_op jit(solution)/shard_map/ppermute | solution.py:28
  171.8 1.1 collective-permute-start.14
  173.6 4.2 %collective-permute-done.14 = f32[4,32,128]{2,1,0:T(8,128)S(1)} collective-permute-done((f32[4,32,128]{2,1,0:T(8,128)S(1)}, f32[4,32,128]{2,1,0:T(8,128)S(1)}, u32[]{:S(2)}, u32[]{:S(2)}) %collective-permute-start.14) | collective-permute-done | bytes 65568 | tf_op jit(solution)/shard_map/ppermute | solution.py:28
  177.8 3.5 %collective-permute-start.15 = (f32[2,32,128]{2,1,0:T(8,128)S(1)}, f32[2,32,128]{2,1,0:T(8,128)S(1)}, u32[]{:S(2)}, u32[]{:S(2)}) collective-permute-start(f32[2,32,128]{2,1,0:T(8,128)S(1)} %constant_dynamic-slice_fusion.1), channel_id=1, source_target_pairs={{0,128},{4,132},{8,136},{12,140},{16,144},{20,148},{24,152},{28,15... | collective-permute-start | bytes 98312 | tf_op jit(solution)/shard_map/ppermute | solution.py:28
  181.3 1.3 exponential_reduce_fusion
  183.4 4.3 %collective-permute-start.16 = (f32[1,32,128]{2,1,0:T(8,128)S(1)}, f32[1,32,128]{2,1,0:T(8,128)S(1)}, u32[]{:S(2)}, u32[]{:S(2)}) collective-permute-start(f32[1,32,128]{2,1,0:T(8,128)S(1)} %constant_dynamic-slice_fusion), channel_id=1, source_target_pairs={{0,32},{4,36},{8,40},{12,44},{16,48},{20,52},{24,56},{28,60},{32,0... | collective-permute-start | bytes 49160 | tf_op jit(solution)/shard_map/ppermute | solution.py:28
  188.4 2.7 %collective-permute-done.16 = f32[1,32,128]{2,1,0:T(8,128)S(1)} collective-permute-done((f32[1,32,128]{2,1,0:T(8,128)S(1)}, f32[1,32,128]{2,1,0:T(8,128)S(1)}, u32[]{:S(2)}, u32[]{:S(2)}) %collective-permute-start.16) | collective-permute-done | bytes 16416 | tf_op jit(solution)/shard_map/ppermute | solution.py:28
  191.8 1.3 exponential_reduce_fusion.1
  193.7 2.4 multiply_reduce_fusion.2
  196.2 1.3 collective-permute-done.17
  198.8 1.7 collective-permute-start.18
  200.4 2.4 collective-permute-done.18
  203.4 3.1 %collective-permute-start.19 = (f32[]{:T(128)}, f32[]{:T(128)}, u32[]{:S(2)}, u32[]{:S(2)}) collective-permute-start(f32[]{:T(128)} %add.207), channel_id=1, source_target_pairs={{0,64},{4,68},{8,72},{12,76},{16,80},{20,84},{24,88},{28,92},{32,9... | collective-permute-start | bytes 20 | tf_op jit(solution)/shard_map/ppermute | solution.py:28
  207.7 1.8 collective-permute-start.20
  209.5 2.9 %collective-permute-done.20 = f32[]{:T(128)} collective-permute-done((f32[]{:T(128)}, f32[]{:T(128)}, u32[]{:S(2)}, u32[]{:S(2)}) %collective-permute-start.20) | collective-permute-done | bytes 36 | tf_op jit(solution)/shard_map/ppermute | solution.py:28
  212.9 4.7 %collective-permute-start.21 = (f32[]{:T(128)}, f32[]{:T(128)}, u32[]{:S(2)}, u32[]{:S(2)}) collective-permute-start(f32[]{:T(128)} %add.209), channel_id=1, source_target_pairs={{0,128},{4,132},{8,136},{12,140},{16,144},{20,148},{24,152},{28,15... | collective-permute-start | bytes 20 | tf_op jit(solution)/shard_map/ppermute | solution.py:28
  218.7 5.6 %collective-permute-start.22 = (f32[]{:T(128)}, f32[]{:T(128)}, u32[]{:S(2)}, u32[]{:S(2)}) collective-permute-start(f32[]{:T(128)} %add.210), channel_id=1, source_target_pairs={{0,32},{4,36},{8,40},{12,44},{16,48},{20,52},{24,56},{28,60},{32,0... | collective-permute-start | bytes 20 | tf_op jit(solution)/shard_map/ppermute | solution.py:28
  224.4 2.0 collective-permute-done.22
  227.0 6.5 %collective-permute-start.23 = (f32[]{:T(128)}, f32[]{:T(128)}, u32[]{:S(2)}, u32[]{:S(2)}) collective-permute-start(f32[]{:T(128)} %add.211), channel_id=1, source_target_pairs={{0,1},{1,0},{2,3},{3,2},{4,5},{5,4},{6,7},{7,6},{8,9},{9,8},{10,11... | collective-permute-start | bytes 20 | tf_op jit(solution)/shard_map/ppermute | solution.py:28
  234.4 2.9 %collective-permute-start.24 = (f32[]{:T(128)}, f32[]{:T(128)}, u32[]{:S(2)}, u32[]{:S(2)}) collective-permute-start(f32[]{:T(128)} %add.212), channel_id=1, source_target_pairs={{0,2},{1,3},{2,0},{3,1},{4,6},{5,7},{6,4},{7,5},{8,10},{9,11},{10,... | collective-permute-start | bytes 20 | tf_op jit(solution)/shard_map/ppermute | solution.py:28
  237.3 2.3 collective-permute-done.24
  (90 shorter events, 9.0 us)
Async XLA Ops:
  7.2 2.3 copy-start
  7.2 129.3 %all-gather.2.cloned.1.call-start = ((), (), s32[]{:S(2)}) async-start(), calls=%async_computation | async-start | bytes 8519680 | tf_op jit(solution)/shard_map/all_gather | solution.py:160
  9.4 2.2 copy-start.4
  9.5 2.2 copy-start.13
  9.5 2.2 copy-start.14
  12.5 15.6 %copy-start.9 = (s32[128]{0:T(128)S(1)}, s32[128]{0:T(128)}, u32[]{:S(2)}) copy-start(s32[128]{0:T(128)} %param.21) | copy-start | bytes 1540
  12.5 16.0 %copy-start.11 = (s32[9]{0:T(128)S(1)}, s32[9]{0:T(128)}, u32[]{:S(2)}) copy-start(s32[9]{0:T(128)} %constant.116.clone) | copy-start | bytes 112
  13.9 14.7 %collective-permute-start = (bf16[2,4,256,128]{3,2,1,0:T(8,128)(2,1)}, bf16[2,4,256,128]{3,2,1,0:T(8,128)(2,1)S(1)}, u32[]{:S(2)}, u32[]{:S(2)}) collective-permute-start(bf16[2,4,256,128]{3,2,1,0:T(8,128)(2,1)} %get-tuple-element.10), channel_id=1, source_target_pairs={{8,4},{4,8},{16,12},{12,16},{24,20},{20,24},{32,28},{28,32},{40,36... | collective-permute-start | bytes 1572872 | tf_op jit(solution)/shard_map/ppermute | solution.py:23
  14.6 23.0 %collective-permute-start.1 = (bf16[2,4,256,128]{3,2,1,0:T(8,128)(2,1)}, bf16[2,4,256,128]{3,2,1,0:T(8,128)(2,1)S(1)}, u32[]{:S(2)}, u32[]{:S(2)}) collective-permute-start(bf16[2,4,256,128]{3,2,1,0:T(8,128)(2,1)} %get-tuple-element.10), channel_id=1, source_target_pairs={{12,4},{0,8},{20,12},{8,16},{28,20},{16,24},{36,28},{24,32},{44,36... | collective-permute-start | bytes 1572872 | tf_op jit(solution)/shard_map/ppermute | solution.py:23
  19.7 20.1 %collective-permute-start.2 = (bf16[2,4,256,128]{3,2,1,0:T(8,128)(2,1)}, bf16[2,4,256,128]{3,2,1,0:T(8,128)(2,1)S(1)}, u32[]{:S(2)}, u32[]{:S(2)}) collective-permute-start(bf16[2,4,256,128]{3,2,1,0:T(8,128)(2,1)} %get-tuple-element.10), channel_id=1, source_target_pairs={{16,4},{24,12},{4,16},{32,20},{12,24},{40,28},{20,32},{48,36},{28,... | collective-permute-start | bytes 1572872 | tf_op jit(solution)/shard_map/ppermute | solution.py:23
  20.4 44.3 %collective-permute-start.3 = (bf16[2,4,256,128]{3,2,1,0:T(8,128)(2,1)}, bf16[2,4,256,128]{3,2,1,0:T(8,128)(2,1)}, u32[]{:S(2)}, u32[]{:S(2)}) collective-permute-start(bf16[2,4,256,128]{3,2,1,0:T(8,128)(2,1)} %get-tuple-element.10), channel_id=1, source_target_pairs={{20,4},{28,12},{0,16},{36,20},{8,24},{44,28},{16,32},{52,36},{24,4... | collective-permute-start | bytes 1572872 | tf_op jit(solution)/shard_map/ppermute | solution.py:23
  27.6 57.4 %collective-permute-start.10 = (bf16[512,2048]{1,0:T(8,128)(2,1)}, bf16[512,2048]{1,0:T(8,128)(2,1)}, u32[]{:S(2)}, u32[]{:S(2)}) collective-permute-start(bf16[512,2048]{1,0:T(8,128)(2,1)} %param.16), channel_id=1, source_target_pairs={{0,3},{1,0},{2,1},{3,2},{4,7},{5,4},{6,5},{7,6},{8,11},{9,8},{10,9... | collective-permute-start | bytes 6291464 | tf_op jit(solution)/shard_map/ppermute | solution.py:33
  28.6 98.0 %collective-permute-start.8 = (bf16[512,2048]{1,0:T(8,128)(2,1)}, bf16[512,2048]{1,0:T(8,128)(2,1)}, u32[]{:S(2)}, u32[]{:S(2)}) collective-permute-start(bf16[512,2048]{1,0:T(8,128)(2,1)} %param.16), channel_id=1, source_target_pairs={{0,1},{1,2},{2,3},{3,0},{4,5},{5,6},{6,7},{7,4},{8,9},{9,10},{10,1... | collective-permute-start | bytes 6291464 | tf_op jit(solution)/shard_map/ppermute | solution.py:33
  37.7 88.9 %collective-permute-start.9 = (bf16[512,2048]{1,0:T(8,128)(2,1)}, bf16[512,2048]{1,0:T(8,128)(2,1)}, u32[]{:S(2)}, u32[]{:S(2)}) collective-permute-start(bf16[512,2048]{1,0:T(8,128)(2,1)} %param.16), channel_id=1, source_target_pairs={{0,2},{1,3},{2,0},{3,1},{4,6},{5,7},{6,4},{7,5},{8,10},{9,11},{10,... | collective-permute-start | bytes 6291464 | tf_op jit(solution)/shard_map/ppermute | solution.py:33
  39.8 0.8 copy-start.2
  42.2 24.5 %collective-permute-start.4 = (bf16[4,2,4,256,128]{4,3,2,1,0:T(8,128)(2,1)}, bf16[4,2,4,256,128]{4,3,2,1,0:T(8,128)(2,1)S(1)}, u32[]{:S(2)}, u32[]{:S(2)}) collective-permute-start(bf16[4,2,4,256,128]{4,3,2,1,0:T(8,128)(2,1)} %pad_maximum_fusion), channel_id=1, source_target_pairs={{0,4},{4,0},{8,12},{12,8},{16,20},{20,16},{24,28},{28,24},{32,36},... | collective-permute-start | bytes 6291464 | tf_op jit(solution)/shard_map/ppermute | solution.py:117
  60.1 3.7 %copy-start.3 = (bf16[2,4,256,128]{3,2,1,0:T(8,128)(2,1)S(1)}, bf16[2,4,256,128]{3,2,1,0:T(8,128)(2,1)}, u32[]{:S(2)}) copy-start(bf16[2,4,256,128]{3,2,1,0:T(8,128)(2,1)} %copy-done.2) | copy-start | bytes 1572868
  66.6 3.6 %copy-start.7 = (pred[256,2304]{1,0:T(8,128)(4,1)S(1)}, pred[256,2304]{1,0:T(8,128)(4,1)}, u32[]{:S(2)}) copy-start(pred[256,2304]{1,0:T(8,128)(4,1)} %fusion.18) | copy-start | bytes 1769476
  75.1 56.1 %copy-start.5 = (bf16[256,2048]{1,0:T(8,128)(2,1)S(1)}, bf16[256,2048]{1,0:T(8,128)(2,1)}, u32[]{:S(2)}) copy-start(bf16[256,2048]{1,0:T(8,128)(2,1)} %param.12) | copy-start | bytes 3145732
  81.9 46.8 %collective-permute-start.5 = (bf16[256,512]{0,1:T(8,128)(2,1)S(1)}, bf16[256,512]{0,1:T(8,128)(2,1)S(1)}, u32[]{:S(2)}, u32[]{:S(2)}) collective-permute-start(bf16[256,512]{0,1:T(8,128)(2,1)S(1)} %bitcast.137), channel_id=1, source_target_pairs={{0,1},{1,2},{2,3},{3,0},{4,5},{5,6},{6,7},{7,4},{8,9},{9,10},{10,1... | collective-permute-start | bytes 786440 | tf_op jit(solution)/shard_map/ppermute | solution.py:33
  83.9 44.8 %collective-permute-start.6 = (bf16[256,512]{0,1:T(8,128)(2,1)S(1)}, bf16[256,512]{0,1:T(8,128)(2,1)S(1)}, u32[]{:S(2)}, u32[]{:S(2)}) collective-permute-start(bf16[256,512]{0,1:T(8,128)(2,1)S(1)} %bitcast.138), channel_id=1, source_target_pairs={{0,2},{1,3},{2,0},{3,1},{4,6},{5,7},{6,4},{7,5},{8,10},{9,11},{10,... | collective-permute-start | bytes 786440 | tf_op jit(solution)/shard_map/ppermute | solution.py:33
  85.0 46.2 %collective-permute-start.7 = (bf16[256,512]{0,1:T(8,128)(2,1)S(1)}, bf16[256,512]{0,1:T(8,128)(2,1)S(1)}, u32[]{:S(2)}, u32[]{:S(2)}) collective-permute-start(bf16[256,512]{0,1:T(8,128)(2,1)S(1)} %bitcast.139), channel_id=1, source_target_pairs={{0,3},{1,0},{2,1},{3,2},{4,7},{5,4},{6,5},{7,6},{8,11},{9,8},{10,9... | collective-permute-start | bytes 786440 | tf_op jit(solution)/shard_map/ppermute | solution.py:33
  126.6 9.6 %copy-start.8 = (f32[2048]{0:T(1024)S(1)}, f32[2048]{0:T(1024)}, u32[]{:S(2)}) copy-start(f32[2048]{0:T(1024)} %param.18) | copy-start | bytes 24580
  136.4 6.1 %copy-start.6 = (bf16[256,2048]{1,0:T(8,128)(2,1)}, bf16[256,2048]{1,0:T(8,128)(2,1)S(1)}, u32[]{:S(2)}) copy-start(bf16[256,2048]{1,0:T(8,128)(2,1)S(1)} %multiply_convert_fusion) | copy-start | bytes 3145732
  148.5 24.4 %copy-start.12 = (f32[1,128]{1,0:T(1,128)S(1)}, f32[1,128]{1,0:T(1,128)}, u32[]{:S(2)}) copy-start(f32[1,128]{1,0:T(1,128)} %param.22) | copy-start | bytes 1540
  148.5 2.3 collective-permute-start.11
  148.5 91.7 %copy-start.1 = (bf16[2048,512]{1,0:T(8,128)(2,1)S(1)}, bf16[2048,512]{1,0:T(8,128)(2,1)}, u32[]{:S(2)}) copy-start(bf16[2048,512]{1,0:T(8,128)(2,1)} %param.14) | copy-start | bytes 6291460
  153.6 9.8 %collective-permute-start.12 = (f32[16,32,128]{2,1,0:T(8,128)S(1)}, f32[16,32,128]{2,1,0:T(8,128)S(1)}, u32[]{:S(2)}, u32[]{:S(2)}) collective-permute-start(f32[16,32,128]{2,1,0:T(8,128)S(1)} %constant_dynamic-slice_fusion.4), channel_id=1, source_target_pairs={{0,8},{4,12},{8,0},{12,4},{16,24},{20,28},{24,16},{28,20},{32,40},... | collective-permute-start | bytes 786440 | tf_op jit(solution)/shard_map/ppermute | solution.py:28
  164.5 7.3 %collective-permute-start.13 = (f32[8,32,128]{2,1,0:T(8,128)S(1)}, f32[8,32,128]{2,1,0:T(8,128)S(1)}, u32[]{:S(2)}, u32[]{:S(2)}) collective-permute-start(f32[8,32,128]{2,1,0:T(8,128)S(1)} %constant_dynamic-slice_fusion.3), channel_id=1, source_target_pairs={{0,64},{4,68},{8,72},{12,76},{16,80},{20,84},{24,88},{28,92},{32,9... | collective-permute-start | bytes 393224 | tf_op jit(solution)/shard_map/ppermute | solution.py:28
  171.8 6.0 %collective-permute-start.14 = (f32[4,32,128]{2,1,0:T(8,128)S(1)}, f32[4,32,128]{2,1,0:T(8,128)S(1)}, u32[]{:S(2)}, u32[]{:S(2)}) collective-permute-start(f32[4,32,128]{2,1,0:T(8,128)S(1)} %constant_dynamic-slice_fusion.2), channel_id=1, source_target_pairs={{0,16},{4,20},{8,24},{12,28},{16,0},{20,4},{24,8},{28,12},{32,48},... | collective-permute-start | bytes 196616 | tf_op jit(solution)/shard_map/ppermute | solution.py:28
  177.8 5.5 %collective-permute-start.15 = (f32[2,32,128]{2,1,0:T(8,128)S(1)}, f32[2,32,128]{2,1,0:T(8,128)S(1)}, u32[]{:S(2)}, u32[]{:S(2)}) collective-permute-start(f32[2,32,128]{2,1,0:T(8,128)S(1)} %constant_dynamic-slice_fusion.1), channel_id=1, source_target_pairs={{0,128},{4,132},{8,136},{12,140},{16,144},{20,148},{24,152},{28,15... | collective-permute-start | bytes 98312 | tf_op jit(solution)/shard_map/ppermute | solution.py:28
  183.4 7.7 %collective-permute-start.16 = (f32[1,32,128]{2,1,0:T(8,128)S(1)}, f32[1,32,128]{2,1,0:T(8,128)S(1)}, u32[]{:S(2)}, u32[]{:S(2)}) collective-permute-start(f32[1,32,128]{2,1,0:T(8,128)S(1)} %constant_dynamic-slice_fusion), channel_id=1, source_target_pairs={{0,32},{4,36},{8,40},{12,44},{16,48},{20,52},{24,56},{28,60},{32,0... | collective-permute-start | bytes 49160 | tf_op jit(solution)/shard_map/ppermute | solution.py:28
  191.8 48.4 %copy-start.10 = (f32[128]{0:T(128)}, f32[128]{0:T(128)S(1)}, u32[]{:S(2)}) copy-start(f32[128]{0:T(128)S(1)} %get-tuple-element.7) | copy-start | bytes 1540
  196.2 1.4 collective-permute-start.17
  198.8 4.0 %collective-permute-start.18 = (f32[]{:T(128)}, f32[]{:T(128)}, u32[]{:S(2)}, u32[]{:S(2)}) collective-permute-start(f32[]{:T(128)} %add.206), channel_id=1, source_target_pairs={{0,8},{4,12},{8,0},{12,4},{16,24},{20,28},{24,16},{28,20},{32,40},... | collective-permute-start | bytes 20 | tf_op jit(solution)/shard_map/ppermute | solution.py:28
  203.4 3.8 %collective-permute-start.19 = (f32[]{:T(128)}, f32[]{:T(128)}, u32[]{:S(2)}, u32[]{:S(2)}) collective-permute-start(f32[]{:T(128)} %add.207), channel_id=1, source_target_pairs={{0,64},{4,68},{8,72},{12,76},{16,80},{20,84},{24,88},{28,92},{32,9... | collective-permute-start | bytes 20 | tf_op jit(solution)/shard_map/ppermute | solution.py:28
  207.7 4.7 %collective-permute-start.20 = (f32[]{:T(128)}, f32[]{:T(128)}, u32[]{:S(2)}, u32[]{:S(2)}) collective-permute-start(f32[]{:T(128)} %add.208), channel_id=1, source_target_pairs={{0,16},{4,20},{8,24},{12,28},{16,0},{20,4},{24,8},{28,12},{32,48},... | collective-permute-start | bytes 20 | tf_op jit(solution)/shard_map/ppermute | solution.py:28
  212.9 5.3 %collective-permute-start.21 = (f32[]{:T(128)}, f32[]{:T(128)}, u32[]{:S(2)}, u32[]{:S(2)}) collective-permute-start(f32[]{:T(128)} %add.209), channel_id=1, source_target_pairs={{0,128},{4,132},{8,136},{12,140},{16,144},{20,148},{24,152},{28,15... | collective-permute-start | bytes 20 | tf_op jit(solution)/shard_map/ppermute | solution.py:28
  218.7 7.7 %collective-permute-start.22 = (f32[]{:T(128)}, f32[]{:T(128)}, u32[]{:S(2)}, u32[]{:S(2)}) collective-permute-start(f32[]{:T(128)} %add.210), channel_id=1, source_target_pairs={{0,32},{4,36},{8,40},{12,44},{16,48},{20,52},{24,56},{28,60},{32,0... | collective-permute-start | bytes 20 | tf_op jit(solution)/shard_map/ppermute | solution.py:28
  227.0 6.8 %collective-permute-start.23 = (f32[]{:T(128)}, f32[]{:T(128)}, u32[]{:S(2)}, u32[]{:S(2)}) collective-permute-start(f32[]{:T(128)} %add.211), channel_id=1, source_target_pairs={{0,1},{1,0},{2,3},{3,2},{4,5},{5,4},{6,7},{7,6},{8,9},{9,8},{10,11... | collective-permute-start | bytes 20 | tf_op jit(solution)/shard_map/ppermute | solution.py:28
  234.4 5.3 %collective-permute-start.24 = (f32[]{:T(128)}, f32[]{:T(128)}, u32[]{:S(2)}, u32[]{:S(2)}) collective-permute-start(f32[]{:T(128)} %add.212), channel_id=1, source_target_pairs={{0,2},{1,3},{2,0},{3,1},{4,6},{5,7},{6,4},{7,5},{8,10},{9,11},{10,... | collective-permute-start | bytes 20 | tf_op jit(solution)/shard_map/ppermute | solution.py:28
Sparse Core Ops, SparseCore 0:
  10.8 95.6 all-gather.1
